TPU v7x, 32 devices: a whole 2x2x4 slice. The times are simulated.
32 devices in a mesh: region: 8 (over y, x, core), dom: 4 (over z).
Axes of the slice: x: 2, y: 2, z: 4, core: 2. Of those that a mesh axis runs over, the one named last changes fastest.
Arguments:
- feats: bfloat16 [16384, 512], P(('region', 'dom')), may hold values from -6 to 6
- hub_feats: bfloat16 [64, 512], P('region'), may hold values from -6 to 6
- hub_ids: int32 [16384, 4], P(('region', 'dom')), may hold values from 0 to 63
- tile_src: int32 [512], P(('region', 'dom')), may hold values from 0 to 4
- tile_mask: int32 [512, 128, 128], P(('region', 'dom')), may hold values 0 or 1
- w_stack: bfloat16 [1024, 512], replicated, may hold values from -0.1875 to 0.1875
- cotangent: bfloat16 [16384, 512], P(('region', 'dom')), may hold values from -6 to 6
Outputs:
- activ: bfloat16 [16384, 512], P(('region', 'dom'))
- weight_grad: float32 [1024, 512], P('dom')
- hub_grad: float32 [64, 512], P('region')
Inputs may be any that keep to these rules, and one draw needn't show every extreme that they name: tile_src names a block of the part's window: 0 is the block taken from the previous part, 1 to 4 are the part's own blocks. `hub_ids`: hub ids index rows of hub_feats.
All inputs are finite; a program needn't handle non-finite values. No bound on the sum of `tile_mask` on one device may be relied on, other than what follows from the above.
Results may differ from a plain program's by a relative error of at most 0.0051.
Values may be sent and summed in bfloat16 or wider, within the bound.
No kernel may reach another device: no remote copies, remote signals or barrier semaphores. Data moves between devices by JAX's collectives and lax.ppermute only.
A program may use at most 64 MiB of HBM per device.

v0:
```python
import jax
import jax.numpy as jnp
from jax import lax
from jax.sharding import PartitionSpec as P


def shifted(value, axis, steps):
    count = lax.axis_size(axis)
    initial, last = (max(0, -steps), min(count, count - steps))
    return lax.ppermute(value, axis, [(source, source + steps) for source in range(initial, last)])


def log2(n):
    bits = n.bit_length() - 1
    assert (1 << bits) == n
    return bits


def exchange(sends, axis, pairs, wire=None):
    width = sends[0].shape[-1]
    flat = jnp.concatenate([x.reshape(-1, width) for x in sends], axis=0)
    kind = flat.dtype
    flat = flat if wire is None else flat.astype(wire)
    flat = lax.ppermute(flat, axis, pairs).astype(kind)
    got, start = [], 0
    for x in sends:
        size = x.size // width
        got.append(flat[start : start + size].reshape(x.shape))
        start += size
    return got


def scatter_sum(values, axis, ats, order, other=None, riders=(), joins=None, wires=None):
    count = lax.axis_size(axis)
    levels = log2(count)
    me = lax.axis_index(axis)
    other = order if other is None else other
    joins = [0] * len(values) if joins is None else joins
    first = (me & 1) == 0
    values = [
        v.reshape(v.shape[:at] + (2,) * levels + v.shape[at + 1 :]) for v, at in zip(values, ats)
    ]
    riders = list(riders)
    held = [[[levels - 1 - k for k in range(levels)] for _ in range(2)] for _ in values]
    for step, (bit, bit_b) in enumerate(zip(order, other)):
        active = [i for i in range(len(values)) if joins[i] <= step]
        keeps, sends = [], []
        for i in active:
            v, at = values[i], ats[i]
            terms = v if isinstance(v, tuple) else (v,)
            parts = []
            for group, b in enumerate((bit, bit_b)):
                dim = at + held[i][group].index(b)
                held[i][group].remove(b)
                mine = (me >> b) & 1
                keep = sum_of([lax.dynamic_index_in_dim(t, mine, axis=dim, keepdims=False) for t in terms])
                send = sum_of([lax.dynamic_index_in_dim(t, 1 - mine, axis=dim, keepdims=False) for t in terms])
                parts.append((keep, send))
            if bit == bit_b:
                keeps.append(parts[0][0])
                sends.append(parts[0][1])
            else:
                keeps.append(jnp.where(first, parts[0][0], parts[1][0]))
                sends.append(jnp.where(first, parts[0][1], parts[1][1]))
        pairs = [(i, i ^ (1 << (bit if i & 1 == 0 else bit_b))) for i in range(count)]
        got = exchange(sends + riders, axis, pairs, None if wires is None else wires[step])
        for i, k, g in zip(active, keeps, got):
            values[i] = (k, g)
        riders = [r + g for r, g in zip(riders, got[len(keeps) :])]
    values = [sum_of(v) if isinstance(v, tuple) else v for v in values]
    return values, riders


def sum_of(terms):
    total = terms[0]
    for t in terms[1:]:
        total = total + t
    return total


def gather_ordered(value, axis, order, rider=None):
    count = lax.axis_size(axis)
    levels = log2(count)
    me = lax.axis_index(axis)
    rest = value.shape
    held = []
    for bit in order:
        pairs = [(i, i ^ (1 << bit)) for i in range(count)]
        mine = (me >> bit) & 1
        if rider is not None and bit == 0:
            keep = lax.dynamic_index_in_dim(rider, mine, axis=0, keepdims=False)
            send = lax.dynamic_index_in_dim(rider, 1 - mine, axis=0, keepdims=False)
            got, got_rider = exchange([value, send], axis, pairs)
            rider = keep + got_rider
        else:
            got = lax.ppermute(value, axis, pairs)
        low = jnp.where(mine == 0, value, got)
        high = jnp.where(mine == 0, got, value)
        value = jnp.stack([low, high], axis=len(held))
        held.append(bit)
    natural = [held.index(levels - 1 - k) for k in range(levels)]
    if natural != list(range(levels)):
        value = jnp.transpose(value, natural + list(range(levels, levels + len(rest))))
    return value.reshape((count,) + rest), rider


def layer(feats, hub_feats, hub_ids, tile_src, tile_mask, w_stack, cotangent):
    rows, width = feats.shape
    tile = tile_mask.shape[1]
    nblk = rows // tile
    per_block = tile_src.shape[0] // nblk
    hub_count = hub_ids.shape[1]
    owned = hub_feats.shape[0]
    regions = lax.axis_size("region")
    doms = lax.axis_size("dom")
    total_hubs = owned * regions
    up = list(range(log2(regions)))
    down = up[::-1]
    prev = shifted(feats[rows - tile :], "dom", 1)
    hub_table = gather_ordered(hub_feats, "region", down)[0].reshape(total_hubs, width)
    window = jnp.concatenate([prev, feats], axis=0)
    src = tile_src.reshape(nblk, per_block)
    chosen = src[:, :, None] == lax.broadcasted_iota(jnp.int32, (nblk, per_block, nblk + 1), 2)
    masks = tile_mask.reshape(nblk, per_block, tile, 1, tile)
    links = jnp.where(chosen[:, :, None, :, None], masks, 0).sum(axis=1)
    links = links.reshape(rows, (nblk + 1) * tile)
    nsum = jnp.dot(links.astype(jnp.bfloat16), window, preferred_element_type=jnp.float32)
    cnt = tile_mask.reshape(nblk, per_block, tile, tile).sum(axis=(1, 3)).reshape(rows)
    deg = 1.0 + cnt.astype(jnp.float32) + jnp.float32(hub_count)
    hub_cols = lax.broadcasted_iota(jnp.int32, (rows, total_hubs), 1)
    counts = jnp.zeros((rows, total_hubs), jnp.float32)
    for slot in range(hub_count):
        counts = counts + (hub_ids[:, slot : slot + 1] == hub_cols).astype(jnp.float32)
    counts = counts.astype(jnp.bfloat16)
    hsum = jnp.dot(counts, hub_table, preferred_element_type=jnp.float32)
    agg = ((feats.astype(jnp.float32) + nsum + hsum) / deg[:, None]).astype(jnp.bfloat16)
    inputs = jnp.concatenate([feats, agg], axis=1)
    z = jnp.dot(inputs, w_stack, preferred_element_type=jnp.float32)
    sig = jax.nn.sigmoid(z)
    activ = (z * sig).astype(jnp.bfloat16)
    dz = (cotangent.astype(jnp.float32) * sig * (1.0 + z * (1.0 - sig))).astype(jnp.bfloat16)
    partial_w = lax.dot_general(inputs, dz, (((0,), (0,)), ((), ())), preferred_element_type=jnp.float32)
    span = partial_w.shape[0] // (doms * regions)
    partial_w = partial_w.reshape(doms, regions, span, width)
    dagg = lax.dot_general(
        dz, w_stack[width:], (((1,), (1,)), ((), ())), preferred_element_type=jnp.float32
    )
    sgrad = (dagg / deg[:, None]).astype(jnp.bfloat16)
    partial_h = lax.dot_general(counts, sgrad, (((0,), (0,)), ((), ())), preferred_element_type=jnp.float32)
    partial_h = partial_h.reshape(regions, owned, width)
    (region_w, region_h), _ = scatter_sum(
        [partial_w, partial_h], "region", [1, 0], up, up[:1] + up[1:][::-1], joins=[0, 1],
        wires=[None, jnp.bfloat16] + [None] * (len(up) - 2),
    )
    (piece_w,), (region_h,) = scatter_sum(
        [region_w], "dom", [0], list(range(log2(doms))), riders=[region_h],
        wires=None,
    )
    weight_grad, hub_grad = gather_ordered(piece_w, "region", down, region_h)
    weight_grad = weight_grad.reshape(regions * span, width)
    return (activ, weight_grad, hub_grad)


def solution(mesh):
    placed = (
        P(("region", "dom"), None),
        P("region", None),
        P(("region", "dom"), None),
        P(("region", "dom")),
        P(("region", "dom"), None, None),
        P(),
        P(("region", "dom"), None),
    )
    return jax.shard_map(
        layer,
        mesh=mesh,
        in_specs=placed,
        out_specs=(P(("region", "dom"), None), P("dom", None), P("region", None)),
        check_vma=False,
    )
```

profile of v0, /device:TPU:0, one launch (start us, length us, event | category | flops | bytes accessed | tf_op | source)
XLA Modules:
  0.0 66.3 jit_solution(474462720316109309)
XLA Ops:
  0.6 0.0 copy-start.5
  0.6 0.0 copy-start.1
  0.7 0.0 copy-start
  0.7 0.0 copy-start.4
  0.7 3.1 %collective-permute-start.1 = (bf16[8,512]{1,0:T(8,128)(2,1)}, bf16[8,512]{1,0:T(8,128)(2,1)S(1)}, u32[]{:S(2)}, u32[]{:S(2)}) collective-permute-start(bf16[8,512]{1,0:T(8,128)(2,1)} %param.8), channel_id=1, source_target_pairs={{0,16},{4,20},{8,24},{12,28},{16,0},{20,4},{24,8},{28,12},{1,17},{... | collective-permute-start | bytes 24584 | tf_op jit(solution)/shard_map/ppermute | solution.py:96
  3.7 0.9 %slice.48 = bf16[128,512]{1,0:T(8,128)(2,1)S(1)} slice(bf16[512,512]{1,0:T(8,128)(2,1)} %param.7), slice={[384:512], [0:512]} | slice | bytes 262144 | tf_op jit(solution)/shard_map/slice | solution.py:119
  4.6 4.1 %collective-permute-start = (bf16[128,512]{1,0:T(8,128)(2,1)S(1)}, bf16[128,512]{1,0:T(8,128)(2,1)}, u32[]{:S(2)}, u32[]{:S(2)}) collective-permute-start(bf16[128,512]{1,0:T(8,128)(2,1)S(1)} %slice.48), channel_id=1, source_target_pairs={{0,1},{1,2},{2,3},{4,5},{5,6},{6,7},{8,9},{9,10},{10,11},{12,13},{... | collective-permute-start | bytes 393224 | tf_op jit(solution)/shard_map/ppermute | solution.py:10
  8.8 0.7 %eq.75 = s32[4,4]{1,0:T(4,128)S(1)} reshape(s32[16]{0:T(128)} %param.10) | data formatting | bytes 128 | tf_op jit(solution)/shard_map/eq | solution.py:123
  9.5 0.1 iota_compare_fusion.4
  9.6 1.9 %select_reduce_fusion = s32[4,128,5,128]{3,1,2,0:T(8,128)S(1)} fusion(s32[4,4,128,128]{3,2,1,0:T(8,128)} %bitcast.141, pred[4,4,5]{2,1,0:T(4,128)(4,1)S(1)} %iota_compare_fusion.4), kind=kLoop, calls=%fused_computation | loop fusion | flops 2293760 | bytes 2359376 | tf_op jit(solution)/shard_map/reduce_sum | solution.py:125
  11.5 0.0 collective-permute-done.1
  11.5 0.0 copy-done.5
  11.5 1.6 %collective-permute-start.2 = (bf16[2,8,512]{2,1,0:T(8,128)(2,1)S(1)}, bf16[2,8,512]{2,1,0:T(8,128)(2,1)S(1)}, u32[]{:S(2)}, u32[]{:S(2)}) collective-permute-start(bf16[2,8,512]{2,1,0:T(8,128)(2,1)S(1)} %pad_maximum_fusion.14), channel_id=1, source_target_pairs={{0,8},{4,12},{8,0},{12,4},{16,24},{20,28},{24,16},{28,20},{1,9},{5... | collective-permute-start | bytes 49160 | tf_op jit(solution)/shard_map/ppermute | solution.py:96
  13.1 0.0 copy-done.4
  13.1 0.0 copy-done
  13.1 0.3 reduce_sum.26
  13.5 1.8 %collective-permute-done.2 = bf16[2,8,512]{2,1,0:T(8,128)(2,1)S(1)} collective-permute-done((bf16[2,8,512]{2,1,0:T(8,128)(2,1)S(1)}, bf16[2,8,512]{2,1,0:T(8,128)(2,1)S(1)}, u32[]{:S(2)}, u32[]{:S(2)}) %collective-permute-start.2) | collective-permute-done | bytes 16416 | tf_op jit(solution)/shard_map/ppermute | solution.py:96
  15.4 0.1 collective-permute-start.3
  15.4 0.0 copy-done.1
  15.5 0.2 copy.35
  15.7 0.1 convert_element_type.52
  15.8 0.9 %copy.32 = bf16[4,128,5,128]{1,0,3,2:T(4,128)(2,1)S(1)} copy(bf16[4,128,5,128]{3,1,2,0:T(8,128)(2,1)S(1)} %convert_element_type.52) | data formatting | bytes 1310720 | tf_op jit(solution)/shard_map/convert_element_type | solution.py:127
  16.8 0.0 collective-permute-done.3
  16.8 0.9 %fusion.20 = f32[512,512]{0,1:T(8,128)S(1)} fusion(bf16[64,512]{1,0:T(8,128)(2,1)S(1)} %bitcast.160, s32[512]{0:T(512)S(1)} %bitcast.166, s32[512]{0:T(512)S(1)} %bitcast.168, s32[512]{0:T(512)S(1)} %bitcast.164, s32[512]{0:T(512)S(1)} %bitcast.162), kind=kOutput, calls=%fused_computation.46 | convolution fusion | flops 33947648 | bytes 1122304 | tf_op jit(solution)/shard_map/dot_general | solution.py:135
  17.8 0.0 collective-permute-done
  17.8 0.0 copy-start.6
  17.8 0.0 copy-start.7
  17.8 1.7 %fusion.2 = bf16[512,512]{0,1:T(8,128)(2,1)S(1)} fusion(f32[512,512]{0,1:T(8,128)S(1)} %fusion.20, bf16[512,512]{0,1:T(8,128)(2,1)S(1)} %copy.35, bf16[80,8,4,128]{3,2,1,0:T(4,128)(2,1)S(1)} %bitcast.150, bf16[512,512]{1,0:T(8,128)(2,1)S(1)} %copy-done.1, bf16[128,512]{1,0:T(8,128)(2,1)} %collective-permute-done, f32[512]{0:T(512)S(1)} %add_bitcast_fusion), kind=kOutput, calls=%fused_computation.5 | convolution fusion | flops 338165760 | bytes 3409920 | tf_op jit(solution)/shard_map/dot_general | solution.py:127
  19.5 0.0 copy-done.6
  19.5 0.0 copy-done.7
  19.5 1.9 %multiply_convert_fusion = (bf16[512,512]{1,0:T(8,128)(2,1)S(1)}, bf16[512,512]{1,0:T(8,128)(2,1)}) fusion(bf16[512,512]{1,0:T(8,128)(2,1)S(1)} %copy-done.7, bf16[1024,512]{1,0:T(8,128)(2,1)S(1)} %copy-done.6, bf16[512,512]{0,1:T(8,128)(2,1)S(1)} %fusion.2, bf16[512,512]{0,1:T(8,128)(2,1)S(1)} %copy.35), kind=kOutput, calls=%fused_computation.9 | convolution fusion | flops 542113792 | bytes 3670016 | tf_op jit(solution)/shard_map/dot_general | solution.py:138
  21.4 0.0 copy-start.2
  21.4 0.7 %fusion.5 = f32[1024,512]{1,0:T(8,128)S(1)} fusion(bf16[512,512]{1,0:T(8,128)(2,1)S(1)} %get-tuple-element.7, bf16[512,512]{0,1:T(8,128)(2,1)S(1)} %fusion.2, bf16[512,512]{0,1:T(8,128)(2,1)S(1)} %copy.35), kind=kOutput, calls=%fused_computation.12 | convolution fusion | flops 538968064 | bytes 3670016 | tf_op jit(solution)/shard_map/dot_general | solution.py:142
  22.1 1.1 %constant_dynamic-slice_fusion.7 = f32[4,2,2,1,32,512]{5,4,3,2,1,0:T(8,128)} fusion(f32[4,2,2,2,32,512]{5,4,3,2,1,0:T(8,128)S(1)} %bitcast.136, s32[]{:T(128)S(6)} %select_n.267), kind=kLoop, calls=%fused_computation.86 | loop fusion | bytes 2097156 | tf_op jit(solution)/shard_map/jit(dynamic_index_in_dim)/dynamic_slice | solution.py:57
  23.2 0.0 copy-done.2
  23.2 0.5 collective-permute-start.4
  23.7 1.9 %fusion.4 = f32[64,512]{1,0:T(8,128)S(1)} fusion(bf16[512,512]{1,0:T(8,128)(2,1)} %copy-done.2, bf16[1024,512]{1,0:T(8,128)(2,1)} %param.12, f32[512]{0:T(512)S(1)} %add_bitcast_fusion, s32[512]{0:T(512)S(1)} %bitcast.167, s32[512]{0:T(512)S(1)} %bitcast.169, s32[512]{0:T(512)S(1)} %bitcast.165, s32[512]{0:T(512)S(1)} %bitcast.163), kind=kOutput, calls=%fused_computation.7 | convolution fusion | flops 302907392 | bytes 1189888 | tf_op jit(solution)/shard_map/dot_general | solution.py:149
  25.6 0.0 copy-start.3
  25.8 0.4 collective-permute-done.4
  26.3 0.0 copy-done.3
  26.3 0.1 fusion.14
  26.4 0.7 %pad_maximum_fusion.4 = bf16[288,512]{1,0:T(8,128)(2,1)} fusion(bf16[32,512]{1,0:T(8,128)(2,1)S(1)} %fusion.21, bf16[256,512]{1,0:T(8,128)(2,1)S(1)} %fusion.14), kind=kLoop, calls=%fused_computation.29 | loop fusion | flops 589824 | bytes 589824 | tf_op jit(solution)/shard_map/concatenate | solution.py:21
  27.2 1.5 %collective-permute-start.5 = (bf16[288,512]{1,0:T(8,128)(2,1)}, bf16[288,512]{1,0:T(8,128)(2,1)S(1)}, u32[]{:S(2)}, u32[]{:S(2)}) collective-permute-start(bf16[288,512]{1,0:T(8,128)(2,1)} %pad_maximum_fusion.4), channel_id=1, source_target_pairs={{0,8},{4,20},{8,0},{12,28},{16,24},{20,4},{24,16},{28,12},{1,9},{5... | collective-permute-start | bytes 884744 | tf_op jit(solution)/shard_map/ppermute | solution.py:24
  28.7 0.9 %bitcast_select_fusion = f32[2,2,8,512]{3,2,1,0:T(8,128)S(1)} fusion(f32[2,2,2,8,512]{4,3,2,1,0:T(8,128)} %bitcast.159, s32[]{:T(128)S(6)} %select_n.268, s32[]{:T(128)S(6)} %select_n.263, pred[]{:T(512)S(6)} %eq.93), kind=kLoop, calls=%fused_computation.52 | loop fusion | flops 16384 | bytes 196617 | tf_op jit(solution)/shard_map/jit(_where)/select_n | solution.py:63
  29.6 0.2 fusion.12
  29.8 4.3 %collective-permute-done.5 = bf16[288,512]{1,0:T(8,128)(2,1)S(1)} collective-permute-done((bf16[288,512]{1,0:T(8,128)(2,1)}, bf16[288,512]{1,0:T(8,128)(2,1)S(1)}, u32[]{:S(2)}, u32[]{:S(2)}) %collective-permute-start.5) | collective-permute-done | bytes 294944 | tf_op jit(solution)/shard_map/ppermute | solution.py:24
  34.1 0.1 slice.64
  34.2 0.2 add_select_fusion.1
  34.5 0.6 collective-permute-start.6
  35.1 6.2 %collective-permute-done.6 = f32[144,512]{1,0:T(8,128)S(1)} collective-permute-done((f32[144,512]{1,0:T(8,128)S(1)}, f32[144,512]{1,0:T(8,128)S(1)}, u32[]{:S(2)}, u32[]{:S(2)}) %collective-permute-start.6) | collective-permute-done | bytes 294944 | tf_op jit(solution)/shard_map/ppermute | solution.py:24
  41.4 1.0 %collective-permute-start.7 = (f32[80,512]{1,0:T(8,128)S(1)}, f32[80,512]{1,0:T(8,128)S(1)}, u32[]{:S(2)}, u32[]{:S(2)}) collective-permute-start(f32[80,512]{1,0:T(8,128)S(1)} %pad_maximum_fusion.9), channel_id=1, source_target_pairs={{0,1},{1,0},{2,3},{3,2},{4,5},{5,4},{6,7},{7,6},{8,9},{9,8},{10,11... | collective-permute-start | bytes 491528 | tf_op jit(solution)/shard_map/ppermute | solution.py:24
  42.4 4.4 %collective-permute-done.7 = f32[80,512]{1,0:T(8,128)S(1)} collective-permute-done((f32[80,512]{1,0:T(8,128)S(1)}, f32[80,512]{1,0:T(8,128)S(1)}, u32[]{:S(2)}, u32[]{:S(2)}) %collective-permute-start.7) | collective-permute-done | bytes 163872 | tf_op jit(solution)/shard_map/ppermute | solution.py:24
  46.9 2.0 %collective-permute-start.8 = (f32[48,512]{1,0:T(8,128)S(1)}, f32[48,512]{1,0:T(8,128)S(1)}, u32[]{:S(2)}, u32[]{:S(2)}) collective-permute-start(f32[48,512]{1,0:T(8,128)S(1)} %pad_maximum_fusion.11), channel_id=1, source_target_pairs={{0,2},{1,3},{2,0},{3,1},{4,6},{5,7},{6,4},{7,5},{8,10},{9,11},{10,... | collective-permute-start | bytes 294920 | tf_op jit(solution)/shard_map/ppermute | solution.py:24
  48.9 4.6 %collective-permute-done.8 = f32[48,512]{1,0:T(8,128)S(1)} collective-permute-done((f32[48,512]{1,0:T(8,128)S(1)}, f32[48,512]{1,0:T(8,128)S(1)}, u32[]{:S(2)}, u32[]{:S(2)}) %collective-permute-start.8) | collective-permute-done | bytes 98336 | tf_op jit(solution)/shard_map/ppermute | solution.py:24
  53.5 0.6 collective-permute-start.9
  54.1 3.8 %collective-permute-done.9 = f32[32,512]{1,0:T(8,128)S(1)} collective-permute-done((f32[32,512]{1,0:T(8,128)S(1)}, f32[32,512]{1,0:T(8,128)S(1)}, u32[]{:S(2)}, u32[]{:S(2)}) %collective-permute-start.9) | collective-permute-done | bytes 65568 | tf_op jit(solution)/shard_map/ppermute | solution.py:96
  57.9 1.6 %collective-permute-start.10 = (f32[2,32,512]{2,1,0:T(8,128)S(1)}, f32[2,32,512]{2,1,0:T(8,128)S(1)}, u32[]{:S(2)}, u32[]{:S(2)}) collective-permute-start(f32[2,32,512]{2,1,0:T(8,128)S(1)} %pad_maximum_fusion.10), channel_id=1, source_target_pairs={{0,8},{4,12},{8,0},{12,4},{16,24},{20,28},{24,16},{28,20},{1,9},{5... | collective-permute-start | bytes 393224 | tf_op jit(solution)/shard_map/ppermute | solution.py:96
  59.5 3.4 %collective-permute-done.10 = f32[2,32,512]{2,1,0:T(8,128)S(1)} collective-permute-done((f32[2,32,512]{2,1,0:T(8,128)S(1)}, f32[2,32,512]{2,1,0:T(8,128)S(1)}, u32[]{:S(2)}, u32[]{:S(2)}) %collective-permute-start.10) | collective-permute-done | bytes 131104 | tf_op jit(solution)/shard_map/ppermute | solution.py:96
  62.9 0.1 fusion.23
  63.1 0.1 collective-permute-start.11
  63.1 1.5 %collective-permute-done.11 = f32[136,512]{1,0:T(8,128)S(1)} collective-permute-done((f32[136,512]{1,0:T(8,128)S(1)}, f32[136,512]{1,0:T(8,128)S(1)}, u32[]{:S(2)}, u32[]{:S(2)}) %collective-permute-start.11) | collective-permute-done | bytes 278560 | tf_op jit(solution)/shard_map/ppermute | solution.py:24
  64.7 0.1 fusion.19
  64.8 0.8 %copy.40 = f32[2,2,2,32,512]{4,3,2,1,0:T(8,128)} copy(f32[2,2,2,32,512]{4,3,1,0,2:T(8,128)S(1)} %pad_maximum_fusion.3) | data formatting | bytes 1048576 | tf_op jit(solution)/shard_map/stack | solution.py:99
  65.7 0.6 slice_add_fusion.2
  (38 shorter events, 0.7 us)
Async XLA Ops:
  0.6 10.9 %copy-start.5 = (bf16[8,512]{1,0:T(8,128)(2,1)S(1)}, bf16[8,512]{1,0:T(8,128)(2,1)}, u32[]{:S(2)}) copy-start(bf16[8,512]{1,0:T(8,128)(2,1)} %param.8) | copy-start | bytes 24580
  0.6 14.8 %copy-start.1 = (bf16[512,512]{1,0:T(8,128)(2,1)S(1)}, bf16[512,512]{1,0:T(8,128)(2,1)}, u32[]{:S(2)}) copy-start(bf16[512,512]{1,0:T(8,128)(2,1)} %param.7) | copy-start | bytes 1572868
  0.7 12.5 %copy-start = (s32[16,128,128]{2,1,0:T(8,128)S(1)}, s32[16,128,128]{2,1,0:T(8,128)}, u32[]{:S(2)}) copy-start(s32[16,128,128]{2,1,0:T(8,128)} %param.11) | copy-start | bytes 3145732
  0.7 12.4 %copy-start.4 = (s32[512,4]{0,1:T(4,128)S(1)}, s32[512,4]{0,1:T(4,128)}, u32[]{:S(2)}) copy-start(s32[512,4]{0,1:T(4,128)} %param.9) | copy-start | bytes 24580
  0.7 10.8 %collective-permute-start.1 = (bf16[8,512]{1,0:T(8,128)(2,1)}, bf16[8,512]{1,0:T(8,128)(2,1)S(1)}, u32[]{:S(2)}, u32[]{:S(2)}) collective-permute-start(bf16[8,512]{1,0:T(8,128)(2,1)} %param.8), channel_id=1, source_target_pairs={{0,16},{4,20},{8,24},{12,28},{16,0},{20,4},{24,8},{28,12},{1,17},{... | collective-permute-start | bytes 24584 | tf_op jit(solution)/shard_map/ppermute | solution.py:96
  4.6 13.1 %collective-permute-start = (bf16[128,512]{1,0:T(8,128)(2,1)S(1)}, bf16[128,512]{1,0:T(8,128)(2,1)}, u32[]{:S(2)}, u32[]{:S(2)}) collective-permute-start(bf16[128,512]{1,0:T(8,128)(2,1)S(1)} %slice.48), channel_id=1, source_target_pairs={{0,1},{1,2},{2,3},{4,5},{5,6},{6,7},{8,9},{9,10},{10,11},{12,13},{... | collective-permute-start | bytes 393224 | tf_op jit(solution)/shard_map/ppermute | solution.py:10
  11.5 3.8 %collective-permute-start.2 = (bf16[2,8,512]{2,1,0:T(8,128)(2,1)S(1)}, bf16[2,8,512]{2,1,0:T(8,128)(2,1)S(1)}, u32[]{:S(2)}, u32[]{:S(2)}) collective-permute-start(bf16[2,8,512]{2,1,0:T(8,128)(2,1)S(1)} %pad_maximum_fusion.14), channel_id=1, source_target_pairs={{0,8},{4,12},{8,0},{12,4},{16,24},{20,28},{24,16},{28,20},{1,9},{5... | collective-permute-start | bytes 49160 | tf_op jit(solution)/shard_map/ppermute | solution.py:96
  15.4 1.4 %collective-permute-start.3 = (bf16[2,2,8,512]{3,2,1,0:T(8,128)(2,1)S(1)}, bf16[2,2,8,512]{3,2,1,0:T(8,128)(2,1)S(1)}, u32[]{:S(2)}, u32[]{:S(2)}) collective-permute-start(bf16[2,2,8,512]{3,2,1,0:T(8,128)(2,1)S(1)} %pad_maximum_fusion.13), channel_id=1, source_target_pairs={{0,4},{4,0},{8,12},{12,8},{16,20},{20,16},{24,28},{28,24},{1,5},{5... | collective-permute-start | bytes 98312 | tf_op jit(solution)/shard_map/ppermute | solution.py:96
  17.8 1.7 %copy-start.6 = (bf16[1024,512]{1,0:T(8,128)(2,1)S(1)}, bf16[1024,512]{1,0:T(8,128)(2,1)}, u32[]{:S(2)}) copy-start(bf16[1024,512]{1,0:T(8,128)(2,1)} %param.12) | copy-start | bytes 3145732
  17.8 1.7 %copy-start.7 = (bf16[512,512]{1,0:T(8,128)(2,1)S(1)}, bf16[512,512]{1,0:T(8,128)(2,1)}, u32[]{:S(2)}) copy-start(bf16[512,512]{1,0:T(8,128)(2,1)} %param.13) | copy-start | bytes 1572868
  21.4 1.8 %copy-start.2 = (bf16[512,512]{1,0:T(8,128)(2,1)}, bf16[512,512]{1,0:T(8,128)(2,1)S(1)}, u32[]{:S(2)}) copy-start(bf16[512,512]{1,0:T(8,128)(2,1)S(1)} %get-tuple-element.7) | copy-start | bytes 1572868
  23.2 3.0 %collective-permute-start.4 = (f32[512,512]{1,0:T(8,128)}, f32[512,512]{1,0:T(8,128)S(1)}, u32[]{:S(2)}, u32[]{:S(2)}) collective-permute-start(f32[512,512]{1,0:T(8,128)} %bitcast.18), channel_id=1, source_target_pairs={{0,4},{4,0},{8,12},{12,8},{16,20},{20,16},{24,28},{28,24},{1,5},{5... | collective-permute-start | bytes 3145736 | tf_op jit(solution)/shard_map/ppermute | solution.py:24
  25.6 0.7 %copy-start.3 = (f32[64,512]{1,0:T(8,128)}, f32[64,512]{1,0:T(8,128)S(1)}, u32[]{:S(2)}) copy-start(f32[64,512]{1,0:T(8,128)S(1)} %fusion.4) | copy-start | bytes 393220
  27.2 6.9 %collective-permute-start.5 = (bf16[288,512]{1,0:T(8,128)(2,1)}, bf16[288,512]{1,0:T(8,128)(2,1)S(1)}, u32[]{:S(2)}, u32[]{:S(2)}) collective-permute-start(bf16[288,512]{1,0:T(8,128)(2,1)} %pad_maximum_fusion.4), channel_id=1, source_target_pairs={{0,8},{4,20},{8,0},{12,28},{16,24},{20,4},{24,16},{28,12},{1,9},{5... | collective-permute-start | bytes 884744 | tf_op jit(solution)/shard_map/ppermute | solution.py:24
  34.5 6.8 %collective-permute-start.6 = (f32[144,512]{1,0:T(8,128)S(1)}, f32[144,512]{1,0:T(8,128)S(1)}, u32[]{:S(2)}, u32[]{:S(2)}) collective-permute-start(f32[144,512]{1,0:T(8,128)S(1)} %pad_maximum_fusion.5), channel_id=1, source_target_pairs={{0,16},{4,12},{8,24},{12,4},{16,0},{20,28},{24,8},{28,20},{1,17},{... | collective-permute-start | bytes 884744 | tf_op jit(solution)/shard_map/ppermute | solution.py:24
  41.4 5.4 %collective-permute-start.7 = (f32[80,512]{1,0:T(8,128)S(1)}, f32[80,512]{1,0:T(8,128)S(1)}, u32[]{:S(2)}, u32[]{:S(2)}) collective-permute-start(f32[80,512]{1,0:T(8,128)S(1)} %pad_maximum_fusion.9), channel_id=1, source_target_pairs={{0,1},{1,0},{2,3},{3,2},{4,5},{5,4},{6,7},{7,6},{8,9},{9,8},{10,11... | collective-permute-start | bytes 491528 | tf_op jit(solution)/shard_map/ppermute | solution.py:24
  46.9 6.6 %collective-permute-start.8 = (f32[48,512]{1,0:T(8,128)S(1)}, f32[48,512]{1,0:T(8,128)S(1)}, u32[]{:S(2)}, u32[]{:S(2)}) collective-permute-start(f32[48,512]{1,0:T(8,128)S(1)} %pad_maximum_fusion.11), channel_id=1, source_target_pairs={{0,2},{1,3},{2,0},{3,1},{4,6},{5,7},{6,4},{7,5},{8,10},{9,11},{10,... | collective-permute-start | bytes 294920 | tf_op jit(solution)/shard_map/ppermute | solution.py:24
  53.5 4.3 %collective-permute-start.9 = (f32[32,512]{1,0:T(8,128)S(1)}, f32[32,512]{1,0:T(8,128)S(1)}, u32[]{:S(2)}, u32[]{:S(2)}) collective-permute-start(f32[32,512]{1,0:T(8,128)S(1)} %slice_add_fusion), channel_id=1, source_target_pairs={{0,16},{4,20},{8,24},{12,28},{16,0},{20,4},{24,8},{28,12},{1,17},{... | collective-permute-start | bytes 196616 | tf_op jit(solution)/shard_map/ppermute | solution.py:96
  57.9 5.0 %collective-permute-start.10 = (f32[2,32,512]{2,1,0:T(8,128)S(1)}, f32[2,32,512]{2,1,0:T(8,128)S(1)}, u32[]{:S(2)}, u32[]{:S(2)}) collective-permute-start(f32[2,32,512]{2,1,0:T(8,128)S(1)} %pad_maximum_fusion.10), channel_id=1, source_target_pairs={{0,8},{4,12},{8,0},{12,4},{16,24},{20,28},{24,16},{28,20},{1,9},{5... | collective-permute-start | bytes 393224 | tf_op jit(solution)/shard_map/ppermute | solution.py:96
  63.1 1.6 %collective-permute-start.11 = (f32[136,512]{1,0:T(8,128)S(1)}, f32[136,512]{1,0:T(8,128)S(1)}, u32[]{:S(2)}, u32[]{:S(2)}) collective-permute-start(f32[136,512]{1,0:T(8,128)S(1)} %pad_maximum_fusion.6), channel_id=1, source_target_pairs={{0,4},{4,0},{8,12},{12,8},{16,20},{20,16},{24,28},{28,24},{1,5},{5... | collective-permute-start | bytes 835592 | tf_op jit(solution)/shard_map/ppermute | solution.py:24
where the time goes:
time: 66.6 us; the launch traced here: 66.3 us
  waiting for transfers between devices  30.5 us (46%)
  starting transfers between devices  16.6 us (25%)
  matrix products  7.12 us (11%)
  other arithmetic  5.77 us (9%)
  local copies, waits for them, and re-layouts  5.12 us (8%)
  between operations  1.16 us (2%)
    ppermute x6, waiting for transfers between devices, exchange(): flat = lax.ppermute(flat, axis, pairs).astype(kind)  21.4 us
    ppermute x5, waiting for transfers between devices, gather_ordered(): got = lax.ppermute(value, axis, pairs)  9.05 us
    ppermute x5, starting transfers between devices, gather_ordered(): got = lax.ppermute(value, axis, pairs)  6.82 us
    ppermute x6, starting transfers between devices, exchange(): flat = lax.ppermute(flat, axis, pairs).astype(kind)  5.66 us
    ppermute x1, starting transfers between devices, shifted(): lax.ppermute(value, axis, [(source, source + steps) for source in range(i...  4.13 us
    dot_general x1, matrix products, layer(): z = jnp.dot(inputs, w_stack, preferred_element_type=jnp.float32)  1.92 us
    dot_general x1, matrix products, layer(): lax.dot_general(counts, sgrad, (((0,), (0,)), ((), ())), preferred_elemen...  1.88 us
    reduce_sum x1, other arithmetic, layer(): links = jnp.where(chosen[:, :, None, :, None], masks, 0).sum(axis=1)  1.88 us
  transfers between devices with their start and end apart: 12, of which 9 were waited for; matrix products, arithmetic and copies ran while one was open for 14% of the time, Pallas kernels for 0%

commit v1 on v0

--- a/solution.py
+++ b/solution.py
@@ -47,14 +47,13 @@
         keeps, sends = [], []
         for i in active:
             v, at = values[i], ats[i]
-            terms = v if isinstance(v, tuple) else (v,)
             parts = []
             for group, b in enumerate((bit, bit_b)):
                 dim = at + held[i][group].index(b)
                 held[i][group].remove(b)
                 mine = (me >> b) & 1
-                keep = sum_of([lax.dynamic_index_in_dim(t, mine, axis=dim, keepdims=False) for t in terms])
-                send = sum_of([lax.dynamic_index_in_dim(t, 1 - mine, axis=dim, keepdims=False) for t in terms])
+                keep = lax.dynamic_index_in_dim(v, mine, axis=dim, keepdims=False)
+                send = lax.dynamic_index_in_dim(v, 1 - mine, axis=dim, keepdims=False)
                 parts.append((keep, send))
             if bit == bit_b:
                 keeps.append(parts[0][0])
@@ -65,17 +64,9 @@
         pairs = [(i, i ^ (1 << (bit if i & 1 == 0 else bit_b))) for i in range(count)]
         got = exchange(sends + riders, axis, pairs, None if wires is None else wires[step])
         for i, k, g in zip(active, keeps, got):
-            values[i] = (k, g)
+            values[i] = k + g
         riders = [r + g for r, g in zip(riders, got[len(keeps) :])]
-    values = [sum_of(v) if isinstance(v, tuple) else v for v in values]
     return values, riders
-
-
-def sum_of(terms):
-    total = terms[0]
-    for t in terms[1:]:
-        total = total + t
-    return total
 
 
 def gather_ordered(value, axis, order, rider=None):
@@ -135,7 +126,8 @@
     hsum = jnp.dot(counts, hub_table, preferred_element_type=jnp.float32)
     agg = ((feats.astype(jnp.float32) + nsum + hsum) / deg[:, None]).astype(jnp.bfloat16)
     inputs = jnp.concatenate([feats, agg], axis=1)
-    z = jnp.dot(inputs, w_stack, preferred_element_type=jnp.float32)
+    z_self = jnp.dot(feats, w_stack[:width], preferred_element_type=jnp.float32)
+    z = z_self + jnp.dot(agg, w_stack[width:], preferred_element_type=jnp.float32)
     sig = jax.nn.sigmoid(z)
     activ = (z * sig).astype(jnp.bfloat16)
     dz = (cotangent.astype(jnp.float32) * sig * (1.0 + z * (1.0 - sig))).astype(jnp.bfloat16)
@@ -150,7 +142,7 @@
     partial_h = partial_h.reshape(regions, owned, width)
     (region_w, region_h), _ = scatter_sum(
         [partial_w, partial_h], "region", [1, 0], up, up[:1] + up[1:][::-1], joins=[0, 1],
-        wires=[None, jnp.bfloat16] + [None] * (len(up) - 2),
+        wires=[None] + [jnp.bfloat16] * (len(up) - 1),
     )
     (piece_w,), (region_h,) = scatter_sum(
         [region_w], "dom", [0], list(range(log2(doms))), riders=[region_h],

time: 66.6 us -> 65 us (0.976)
  matrix products: 7.12 us -> 9.53 us
  other arithmetic: 5.77 us -> 3.9 us
  local copies, waits for them, and re-layouts: 5.12 us -> 3.49 us
    dot_general x1 -> x2, matrix products: 1.92 us -> 4.29 us  [the longest x1 2.64 us: layer(): z_self = jnp.dot(feats, w_stack[:width], preferred_element_type=jnp.float32)]
    add x4 -> x7, other arithmetic: 0.09 us -> 1.69 us  [scatter_sum(): values[i] = k + g]
    reduce_sum x1, other arithmetic: 1.88 us -> 0.51 us  [layer(): links = jnp.where(chosen[:, :, None, :, None], masks, 0).sum(axis=1)]
    select_n x3 -> x1, other arithmetic: 1.38 us -> 0.04 us  [scatter_sum(): keeps.append(jnp.where(first, parts[0][0], parts[1][0]))]
    dynamic_slice x8 -> x6, local copies, waits for them, and re-layouts: 1.31 us -> 0.22 us  [scatter_sum(): send = lax.dynamic_index_in_dim(v, 1 - mine, axis=dim, keepdims=False)]
    concatenate x5, other arithmetic: 0.8 us -> 0.08 us  [exchange(): flat = jnp.concatenate([x.reshape(-1, width) for x in sends], axis=0)]
where the time goes in v1:
time: 65 us; the launch traced here: 64.7 us
  waiting for transfers between devices  29.9 us (46%)
  starting transfers between devices  16.7 us (26%)
  matrix products  9.53 us (15%)
  other arithmetic  3.9 us (6%)
  local copies, waits for them, and re-layouts  3.49 us (5%)
  between operations  1.19 us (2%)
    ppermute x6, waiting for transfers between devices, exchange(): flat = lax.ppermute(flat, axis, pairs).astype(kind)  20.9 us
    ppermute x5, waiting for transfers between devices, gather_ordered(): got = lax.ppermute(value, axis, pairs)  9.07 us
    ppermute x5, starting transfers between devices, gather_ordered(): got = lax.ppermute(value, axis, pairs)  6.81 us
    ppermute x6, starting transfers between devices, exchange(): flat = lax.ppermute(flat, axis, pairs).astype(kind)  5.72 us
    ppermute x1, starting transfers between devices, shifted(): lax.ppermute(value, axis, [(source, source + steps) for source in range(i...  4.15 us
    dot_general x1, matrix products, layer(): z_self = jnp.dot(feats, w_stack[:width], preferred_element_type=jnp.float32)  2.64 us
    dot_general x1, matrix products, layer(): lax.dot_general(counts, sgrad, (((0,), (0,)), ((), ())), preferred_elemen...  1.88 us
    dot_general x1, matrix products, layer(): jnp.dot(links.astype(jnp.bfloat16), window, preferred_element_type=jnp.fl...  1.72 us
  transfers between devices with their start and end apart: 12, of which 9 were waited for; matrix products, arithmetic and copies ran while one was open for 14% of the time, Pallas kernels for 0%

profile of v1, /device:TPU:0, one launch (start us, length us, event | category | flops | bytes accessed | tf_op | source)
XLA Modules:
  0.0 64.7 jit_solution(11691063881343123214)
XLA Ops:
  0.6 0.0 copy-start.9
  0.6 0.0 copy-start
  0.7 3.1 %collective-permute-start.1 = (bf16[8,512]{1,0:T(8,128)(2,1)}, bf16[8,512]{1,0:T(8,128)(2,1)S(1)}, u32[]{:S(2)}, u32[]{:S(2)}) collective-permute-start(bf16[8,512]{1,0:T(8,128)(2,1)} %param.8), channel_id=1, source_target_pairs={{0,16},{4,20},{8,24},{12,28},{16,0},{20,4},{24,8},{28,12},{1,17},{... | collective-permute-start | bytes 24584 | tf_op jit(solution)/shard_map/ppermute | solution.py:87
  3.7 0.9 %slice.53 = bf16[128,512]{1,0:T(8,128)(2,1)S(1)} slice(bf16[512,512]{1,0:T(8,128)(2,1)} %param.7), slice={[384:512], [0:512]} | slice | bytes 262144 | tf_op jit(solution)/shard_map/slice | solution.py:110
  4.6 0.0 copy-start.6
  4.6 0.0 copy-start.5
  4.7 4.2 %collective-permute-start = (bf16[128,512]{1,0:T(8,128)(2,1)S(1)}, bf16[128,512]{1,0:T(8,128)(2,1)}, u32[]{:S(2)}, u32[]{:S(2)}) collective-permute-start(bf16[128,512]{1,0:T(8,128)(2,1)S(1)} %slice.53), channel_id=1, source_target_pairs={{0,1},{1,2},{2,3},{4,5},{5,6},{6,7},{8,9},{9,10},{10,11},{12,13},{... | collective-permute-start | bytes 393224 | tf_op jit(solution)/shard_map/ppermute | solution.py:10
  8.8 2.6 %fusion.17 = f32[512,512]{1,0:T(8,128)} fusion(bf16[512,512]{1,0:T(8,128)(2,1)} %param.7, bf16[1024,512]{1,0:T(8,128)(2,1)} %param.12), kind=kOutput, calls=%fused_computation.28 | convolution fusion | flops 268435456 | bytes 2097152 | tf_op jit(solution)/shard_map/dot_general | solution.py:129
  11.4 0.0 copy-done.9
  11.4 0.1 eq.75
  11.5 0.1 iota_compare_fusion.4
  11.6 0.0 copy-done
  11.6 0.5 select_reduce_fusion
  12.1 0.0 collective-permute-done.1
  12.1 0.0 copy-done.6
  12.2 1.6 %collective-permute-start.2 = (bf16[2,8,512]{2,1,0:T(8,128)(2,1)S(1)}, bf16[2,8,512]{2,1,0:T(8,128)(2,1)S(1)}, u32[]{:S(2)}, u32[]{:S(2)}) collective-permute-start(bf16[2,8,512]{2,1,0:T(8,128)(2,1)S(1)} %pad_maximum_fusion.11), channel_id=1, source_target_pairs={{0,8},{4,12},{8,0},{12,4},{16,24},{20,28},{24,16},{28,20},{1,9},{5... | collective-permute-start | bytes 49160 | tf_op jit(solution)/shard_map/ppermute | solution.py:87
  13.7 0.0 copy-done.5
  13.7 0.3 reduce_sum.26
  14.1 1.9 %collective-permute-done.2 = bf16[2,8,512]{2,1,0:T(8,128)(2,1)S(1)} collective-permute-done((bf16[2,8,512]{2,1,0:T(8,128)(2,1)S(1)}, bf16[2,8,512]{2,1,0:T(8,128)(2,1)S(1)}, u32[]{:S(2)}, u32[]{:S(2)}) %collective-permute-start.2) | collective-permute-done | bytes 16416 | tf_op jit(solution)/shard_map/ppermute | solution.py:87
  16.0 0.1 collective-permute-start.3
  16.1 0.0 copy-start.7
  16.1 0.0 copy-done.1
  16.1 0.2 copy.32
  16.3 0.1 convert_element_type.56
  16.5 0.9 %copy.33 = bf16[4,128,5,128]{1,0,3,2:T(4,128)(2,1)S(1)} copy(bf16[4,128,5,128]{3,1,2,0:T(8,128)(2,1)S(1)} %convert_element_type.56) | data formatting | bytes 1310720 | tf_op jit(solution)/shard_map/convert_element_type | solution.py:118
  17.4 0.0 collective-permute-done.3
  17.5 0.9 %fusion.24 = f32[512,512]{0,1:T(8,128)S(1)} fusion(bf16[64,512]{1,0:T(8,128)(2,1)S(1)} %bitcast.138, s32[512]{0:T(512)S(1)} %bitcast.145, s32[512]{0:T(512)S(1)} %bitcast.147, s32[512]{0:T(512)S(1)} %bitcast.143, s32[512]{0:T(512)S(1)} %bitcast.141), kind=kOutput, calls=%fused_computation.50 | convolution fusion | flops 33947648 | bytes 1122304 | tf_op jit(solution)/shard_map/dot_general | solution.py:126
  18.4 0.0 collective-permute-done
  18.4 0.0 copy-done.7
  18.4 0.0 copy-start.4
  18.4 0.0 copy-start.10
  18.5 1.7 %fusion.2 = bf16[512,512]{0,1:T(8,128)(2,1)S(1)} fusion(f32[512,512]{0,1:T(8,128)S(1)} %fusion.24, bf16[512,512]{0,1:T(8,128)(2,1)S(1)} %copy.32, bf16[80,8,4,128]{3,2,1,0:T(4,128)(2,1)S(1)} %bitcast.130, bf16[512,512]{1,0:T(8,128)(2,1)S(1)} %copy-done.1, bf16[128,512]{1,0:T(8,128)(2,1)} %collective-permute-done, f32[512]{0:T(512)S(1)} %add_bitcast_fusion), kind=kOutput, calls=%fused_computation.6 | convolution fusion | flops 338165760 | bytes 3409920 | tf_op jit(solution)/shard_map/dot_general | solution.py:118
  20.2 0.0 copy-done.2
  20.2 0.0 copy-done.4
  20.2 0.0 copy-done.10
  20.2 1.7 %multiply_convert_fusion = (bf16[512,512]{1,0:T(8,128)(2,1)S(1)}, bf16[512,512]{1,0:T(8,128)(2,1)}) fusion(bf16[512,512]{1,0:T(8,128)(2,1)S(1)} %copy-done.10, f32[512,512]{1,0:T(8,128)S(1)} %copy-done.2, bf16[512,512]{0,1:T(8,128)(2,1)S(1)} %fusion.2, bf16[1024,512]{1,0:T(8,128)(2,1)S(1)} %copy-done.4), kind=kOutput, calls=%fused_computation.14 | convolution fusion | flops 271843328 | bytes 3670016 | tf_op jit(solution)/shard_map/dot_general | solution.py:130
  21.9 0.7 %fusion.5 = f32[1024,512]{1,0:T(8,128)S(1)} fusion(bf16[512,512]{1,0:T(8,128)(2,1)S(1)} %get-tuple-element.3, bf16[512,512]{0,1:T(8,128)(2,1)S(1)} %fusion.2, bf16[512,512]{0,1:T(8,128)(2,1)S(1)} %copy.32), kind=kOutput, calls=%fused_computation.9 | convolution fusion | flops 538968064 | bytes 3670016 | tf_op jit(solution)/shard_map/dot_general | solution.py:134
  22.6 0.1 copy-done.3
  22.7 0.1 constant_dynamic-slice_fusion.5
  22.8 0.5 collective-permute-start.4
  23.3 1.9 %fusion.4 = f32[64,512]{1,0:T(8,128)S(1)} fusion(bf16[512,512]{1,0:T(8,128)(2,1)} %copy-done.3, f32[512]{0:T(512)S(1)} %copy-done.8, bf16[1024,512]{1,0:T(8,128)(2,1)} %param.12, s32[512]{0:T(512)S(1)} %bitcast.146, s32[512]{0:T(512)S(1)} %bitcast.148, s32[512]{0:T(512)S(1)} %bitcast.144, s32[512]{0:T(512)S(1)} %bitcast.142), kind=kOutput, calls=%fused_computation.8 | convolution fusion | flops 302907392 | bytes 1189888 | tf_op jit(solution)/shard_map/dot_general | solution.py:141
  25.3 0.5 collective-permute-done.4
  25.7 1.4 %bitcast_add_fusion = f32[4,2,2,32,512]{4,3,2,1,0:T(8,128)S(1)} fusion(f32[4,2,2,32,512]{4,3,2,1,0:T(8,128)} %bitcast.19, f32[4,2,2,2,32,512]{5,4,3,2,1,0:T(8,128)S(1)} %bitcast.122, s32[]{:T(128)S(6)} %select_n.233), kind=kLoop, calls=%fused_computation.13 | loop fusion | flops 262144 | bytes 3145732 | tf_op jit(solution)/shard_map/add | solution.py:67
  27.3 0.1 fusion.14
  27.4 1.6 %collective-permute-start.5 = (bf16[288,512]{1,0:T(8,128)(2,1)S(1)}, bf16[288,512]{1,0:T(8,128)(2,1)S(1)}, u32[]{:S(2)}, u32[]{:S(2)}) collective-permute-start(bf16[288,512]{1,0:T(8,128)(2,1)S(1)} %pad_maximum_fusion.1), channel_id=1, source_target_pairs={{0,8},{4,20},{8,0},{12,28},{16,24},{20,4},{24,16},{28,12},{1,9},{5... | collective-permute-start | bytes 884744 | tf_op jit(solution)/shard_map/ppermute | solution.py:24
  28.9 5.2 %collective-permute-done.5 = bf16[288,512]{1,0:T(8,128)(2,1)S(1)} collective-permute-done((bf16[288,512]{1,0:T(8,128)(2,1)S(1)}, bf16[288,512]{1,0:T(8,128)(2,1)S(1)}, u32[]{:S(2)}, u32[]{:S(2)}) %collective-permute-start.5) | collective-permute-done | bytes 294944 | tf_op jit(solution)/shard_map/ppermute | solution.py:24
  34.2 0.1 slice.69
  34.3 0.2 fusion.15
  34.5 0.6 collective-permute-start.6
  35.1 4.6 %collective-permute-done.6 = bf16[144,512]{1,0:T(8,128)(2,1)S(1)} collective-permute-done((bf16[144,512]{1,0:T(8,128)(2,1)S(1)}, bf16[144,512]{1,0:T(8,128)(2,1)S(1)}, u32[]{:S(2)}, u32[]{:S(2)}) %collective-permute-start.6) | collective-permute-done | bytes 147488 | tf_op jit(solution)/shard_map/ppermute | solution.py:24
  39.9 1.0 %collective-permute-start.7 = (f32[80,512]{1,0:T(8,128)S(1)}, f32[80,512]{1,0:T(8,128)S(1)}, u32[]{:S(2)}, u32[]{:S(2)}) collective-permute-start(f32[80,512]{1,0:T(8,128)S(1)} %pad_maximum_fusion.5), channel_id=1, source_target_pairs={{0,1},{1,0},{2,3},{3,2},{4,5},{5,4},{6,7},{7,6},{8,9},{9,8},{10,11... | collective-permute-start | bytes 491528 | tf_op jit(solution)/shard_map/ppermute | solution.py:24
  40.8 4.4 %collective-permute-done.7 = f32[80,512]{1,0:T(8,128)S(1)} collective-permute-done((f32[80,512]{1,0:T(8,128)S(1)}, f32[80,512]{1,0:T(8,128)S(1)}, u32[]{:S(2)}, u32[]{:S(2)}) %collective-permute-start.7) | collective-permute-done | bytes 163872 | tf_op jit(solution)/shard_map/ppermute | solution.py:24
  45.3 2.0 %collective-permute-start.8 = (f32[48,512]{1,0:T(8,128)S(1)}, f32[48,512]{1,0:T(8,128)S(1)}, u32[]{:S(2)}, u32[]{:S(2)}) collective-permute-start(f32[48,512]{1,0:T(8,128)S(1)} %pad_maximum_fusion.8), channel_id=1, source_target_pairs={{0,2},{1,3},{2,0},{3,1},{4,6},{5,7},{6,4},{7,5},{8,10},{9,11},{10,... | collective-permute-start | bytes 294920 | tf_op jit(solution)/shard_map/ppermute | solution.py:24
  47.3 4.6 %collective-permute-done.8 = f32[48,512]{1,0:T(8,128)S(1)} collective-permute-done((f32[48,512]{1,0:T(8,128)S(1)}, f32[48,512]{1,0:T(8,128)S(1)}, u32[]{:S(2)}, u32[]{:S(2)}) %collective-permute-start.8) | collective-permute-done | bytes 98336 | tf_op jit(solution)/shard_map/ppermute | solution.py:24
  52.0 0.6 collective-permute-start.9
  52.6 3.8 %collective-permute-done.9 = f32[32,512]{1,0:T(8,128)S(1)} collective-permute-done((f32[32,512]{1,0:T(8,128)S(1)}, f32[32,512]{1,0:T(8,128)S(1)}, u32[]{:S(2)}, u32[]{:S(2)}) %collective-permute-start.9) | collective-permute-done | bytes 65568 | tf_op jit(solution)/shard_map/ppermute | solution.py:87
  56.4 1.6 %collective-permute-start.10 = (f32[2,32,512]{2,1,0:T(8,128)S(1)}, f32[2,32,512]{2,1,0:T(8,128)S(1)}, u32[]{:S(2)}, u32[]{:S(2)}) collective-permute-start(f32[2,32,512]{2,1,0:T(8,128)S(1)} %pad_maximum_fusion.7), channel_id=1, source_target_pairs={{0,8},{4,12},{8,0},{12,4},{16,24},{20,28},{24,16},{28,20},{1,9},{5... | collective-permute-start | bytes 393224 | tf_op jit(solution)/shard_map/ppermute | solution.py:87
  57.9 3.4 %collective-permute-done.10 = f32[2,32,512]{2,1,0:T(8,128)S(1)} collective-permute-done((f32[2,32,512]{2,1,0:T(8,128)S(1)}, f32[2,32,512]{2,1,0:T(8,128)S(1)}, u32[]{:S(2)}, u32[]{:S(2)}) %collective-permute-start.10) | collective-permute-done | bytes 131104 | tf_op jit(solution)/shard_map/ppermute | solution.py:87
  61.4 0.1 fusion.28
  61.5 0.1 collective-permute-start.11
  61.6 1.5 %collective-permute-done.11 = f32[136,512]{1,0:T(8,128)S(1)} collective-permute-done((f32[136,512]{1,0:T(8,128)S(1)}, f32[136,512]{1,0:T(8,128)S(1)}, u32[]{:S(2)}, u32[]{:S(2)}) %collective-permute-start.11) | collective-permute-done | bytes 278560 | tf_op jit(solution)/shard_map/ppermute | solution.py:24
  63.2 0.1 fusion.23
  63.3 0.8 %copy.40 = f32[2,2,2,32,512]{4,3,2,1,0:T(8,128)} copy(f32[2,2,2,32,512]{4,3,1,0,2:T(8,128)S(1)} %pad_maximum_fusion) | data formatting | bytes 1048576 | tf_op jit(solution)/shard_map/stack | solution.py:90
  64.1 0.6 slice_add_fusion.2
  (47 shorter events, 0.7 us)
Async XLA Ops:
  0.6 10.8 %copy-start.9 = (s32[16]{0:T(128)S(1)}, s32[16]{0:T(128)}, u32[]{:S(2)}) copy-start(s32[16]{0:T(128)} %param.10) | copy-start | bytes 196
  0.6 11.0 %copy-start = (s32[16,128,128]{2,1,0:T(8,128)S(1)}, s32[16,128,128]{2,1,0:T(8,128)}, u32[]{:S(2)}) copy-start(s32[16,128,128]{2,1,0:T(8,128)} %param.11) | copy-start | bytes 3145732
  0.7 11.5 %collective-permute-start.1 = (bf16[8,512]{1,0:T(8,128)(2,1)}, bf16[8,512]{1,0:T(8,128)(2,1)S(1)}, u32[]{:S(2)}, u32[]{:S(2)}) collective-permute-start(bf16[8,512]{1,0:T(8,128)(2,1)} %param.8), channel_id=1, source_target_pairs={{0,16},{4,20},{8,24},{12,28},{16,0},{20,4},{24,8},{28,12},{1,17},{... | collective-permute-start | bytes 24584 | tf_op jit(solution)/shard_map/ppermute | solution.py:87
  4.6 7.5 %copy-start.6 = (bf16[8,512]{1,0:T(8,128)(2,1)S(1)}, bf16[8,512]{1,0:T(8,128)(2,1)}, u32[]{:S(2)}) copy-start(bf16[8,512]{1,0:T(8,128)(2,1)} %param.8) | copy-start | bytes 24580
  4.6 9.1 %copy-start.5 = (s32[512,4]{0,1:T(4,128)S(1)}, s32[512,4]{0,1:T(4,128)}, u32[]{:S(2)}) copy-start(s32[512,4]{0,1:T(4,128)} %param.9) | copy-start | bytes 24580
  4.7 13.8 %collective-permute-start = (bf16[128,512]{1,0:T(8,128)(2,1)S(1)}, bf16[128,512]{1,0:T(8,128)(2,1)}, u32[]{:S(2)}, u32[]{:S(2)}) collective-permute-start(bf16[128,512]{1,0:T(8,128)(2,1)S(1)} %slice.53), channel_id=1, source_target_pairs={{0,1},{1,2},{2,3},{4,5},{5,6},{6,7},{8,9},{9,10},{10,11},{12,13},{... | collective-permute-start | bytes 393224 | tf_op jit(solution)/shard_map/ppermute | solution.py:10
  11.4 4.7 %copy-start.1 = (bf16[512,512]{1,0:T(8,128)(2,1)S(1)}, bf16[512,512]{1,0:T(8,128)(2,1)}, u32[]{:S(2)}) copy-start(bf16[512,512]{1,0:T(8,128)(2,1)} %param.7) | copy-start | bytes 1572868
  12.2 3.8 %collective-permute-start.2 = (bf16[2,8,512]{2,1,0:T(8,128)(2,1)S(1)}, bf16[2,8,512]{2,1,0:T(8,128)(2,1)S(1)}, u32[]{:S(2)}, u32[]{:S(2)}) collective-permute-start(bf16[2,8,512]{2,1,0:T(8,128)(2,1)S(1)} %pad_maximum_fusion.11), channel_id=1, source_target_pairs={{0,8},{4,12},{8,0},{12,4},{16,24},{20,28},{24,16},{28,20},{1,9},{5... | collective-permute-start | bytes 49160 | tf_op jit(solution)/shard_map/ppermute | solution.py:87
  16.0 1.4 %collective-permute-start.3 = (bf16[2,2,8,512]{3,2,1,0:T(8,128)(2,1)S(1)}, bf16[2,2,8,512]{3,2,1,0:T(8,128)(2,1)S(1)}, u32[]{:S(2)}, u32[]{:S(2)}) collective-permute-start(bf16[2,2,8,512]{3,2,1,0:T(8,128)(2,1)S(1)} %pad_maximum_fusion.10), channel_id=1, source_target_pairs={{0,4},{4,0},{8,12},{12,8},{16,20},{20,16},{24,28},{28,24},{1,5},{5... | collective-permute-start | bytes 98312 | tf_op jit(solution)/shard_map/ppermute | solution.py:87
  16.1 2.3 %copy-start.7 = (f32[512]{0:T(512)}, f32[512]{0:T(512)S(1)}, u32[]{:S(2)}) copy-start(f32[512]{0:T(512)S(1)} %add_bitcast_fusion) | copy-start | bytes 6148
  18.4 1.8 %copy-start.2 = (f32[512,512]{1,0:T(8,128)S(1)}, f32[512,512]{1,0:T(8,128)}, u32[]{:S(2)}) copy-start(f32[512,512]{1,0:T(8,128)} %fusion.17) | copy-start | bytes 3145732
  18.4 1.8 %copy-start.4 = (bf16[1024,512]{1,0:T(8,128)(2,1)S(1)}, bf16[1024,512]{1,0:T(8,128)(2,1)}, u32[]{:S(2)}) copy-start(bf16[1024,512]{1,0:T(8,128)(2,1)} %param.12) | copy-start | bytes 3145732
  18.4 1.8 %copy-start.10 = (bf16[512,512]{1,0:T(8,128)(2,1)S(1)}, bf16[512,512]{1,0:T(8,128)(2,1)}, u32[]{:S(2)}) copy-start(bf16[512,512]{1,0:T(8,128)(2,1)} %param.13) | copy-start | bytes 1572868
  21.9 0.8 %copy-start.3 = (bf16[512,512]{1,0:T(8,128)(2,1)}, bf16[512,512]{1,0:T(8,128)(2,1)S(1)}, u32[]{:S(2)}) copy-start(bf16[512,512]{1,0:T(8,128)(2,1)S(1)} %get-tuple-element.3) | copy-start | bytes 1572868
  21.9 1.4 %copy-start.8 = (f32[512]{0:T(512)S(1)}, f32[512]{0:T(512)}, u32[]{:S(2)}) copy-start(f32[512]{0:T(512)} %copy-done.7) | copy-start | bytes 6148
  22.8 3.0 %collective-permute-start.4 = (f32[512,512]{1,0:T(8,128)S(1)}, f32[512,512]{1,0:T(8,128)}, u32[]{:S(2)}, u32[]{:S(2)}) collective-permute-start(f32[512,512]{1,0:T(8,128)S(1)} %bitcast.125), channel_id=1, source_target_pairs={{0,4},{4,0},{8,12},{12,8},{16,20},{20,16},{24,28},{28,24},{1,5},{5... | collective-permute-start | bytes 3145736 | tf_op jit(solution)/shard_map/ppermute | solution.py:24
  27.4 6.8 %collective-permute-start.5 = (bf16[288,512]{1,0:T(8,128)(2,1)S(1)}, bf16[288,512]{1,0:T(8,128)(2,1)S(1)}, u32[]{:S(2)}, u32[]{:S(2)}) collective-permute-start(bf16[288,512]{1,0:T(8,128)(2,1)S(1)} %pad_maximum_fusion.1), channel_id=1, source_target_pairs={{0,8},{4,20},{8,0},{12,28},{16,24},{20,4},{24,16},{28,12},{1,9},{5... | collective-permute-start | bytes 884744 | tf_op jit(solution)/shard_map/ppermute | solution.py:24
  34.5 5.2 %collective-permute-start.6 = (bf16[144,512]{1,0:T(8,128)(2,1)S(1)}, bf16[144,512]{1,0:T(8,128)(2,1)S(1)}, u32[]{:S(2)}, u32[]{:S(2)}) collective-permute-start(bf16[144,512]{1,0:T(8,128)(2,1)S(1)} %pad_maximum_fusion.6), channel_id=1, source_target_pairs={{0,16},{4,12},{8,24},{12,4},{16,0},{20,28},{24,8},{28,20},{1,17},{... | collective-permute-start | bytes 442376 | tf_op jit(solution)/shard_map/ppermute | solution.py:24
  39.9 5.4 %collective-permute-start.7 = (f32[80,512]{1,0:T(8,128)S(1)}, f32[80,512]{1,0:T(8,128)S(1)}, u32[]{:S(2)}, u32[]{:S(2)}) collective-permute-start(f32[80,512]{1,0:T(8,128)S(1)} %pad_maximum_fusion.5), channel_id=1, source_target_pairs={{0,1},{1,0},{2,3},{3,2},{4,5},{5,4},{6,7},{7,6},{8,9},{9,8},{10,11... | collective-permute-start | bytes 491528 | tf_op jit(solution)/shard_map/ppermute | solution.py:24
  45.3 6.6 %collective-permute-start.8 = (f32[48,512]{1,0:T(8,128)S(1)}, f32[48,512]{1,0:T(8,128)S(1)}, u32[]{:S(2)}, u32[]{:S(2)}) collective-permute-start(f32[48,512]{1,0:T(8,128)S(1)} %pad_maximum_fusion.8), channel_id=1, source_target_pairs={{0,2},{1,3},{2,0},{3,1},{4,6},{5,7},{6,4},{7,5},{8,10},{9,11},{10,... | collective-permute-start | bytes 294920 | tf_op jit(solution)/shard_map/ppermute | solution.py:24
  52.0 4.3 %collective-permute-start.9 = (f32[32,512]{1,0:T(8,128)S(1)}, f32[32,512]{1,0:T(8,128)S(1)}, u32[]{:S(2)}, u32[]{:S(2)}) collective-permute-start(f32[32,512]{1,0:T(8,128)S(1)} %slice_add_fusion), channel_id=1, source_target_pairs={{0,16},{4,20},{8,24},{12,28},{16,0},{20,4},{24,8},{28,12},{1,17},{... | collective-permute-start | bytes 196616 | tf_op jit(solution)/shard_map/ppermute | solution.py:87
  56.4 5.0 %collective-permute-start.10 = (f32[2,32,512]{2,1,0:T(8,128)S(1)}, f32[2,32,512]{2,1,0:T(8,128)S(1)}, u32[]{:S(2)}, u32[]{:S(2)}) collective-permute-start(f32[2,32,512]{2,1,0:T(8,128)S(1)} %pad_maximum_fusion.7), channel_id=1, source_target_pairs={{0,8},{4,12},{8,0},{12,4},{16,24},{20,28},{24,16},{28,20},{1,9},{5... | collective-permute-start | bytes 393224 | tf_op jit(solution)/shard_map/ppermute | solution.py:87
  61.5 1.6 %collective-permute-start.11 = (f32[136,512]{1,0:T(8,128)S(1)}, f32[136,512]{1,0:T(8,128)S(1)}, u32[]{:S(2)}, u32[]{:S(2)}) collective-permute-start(f32[136,512]{1,0:T(8,128)S(1)} %pad_maximum_fusion.2), channel_id=1, source_target_pairs={{0,4},{4,0},{8,12},{12,8},{16,20},{20,16},{24,28},{28,24},{1,5},{5... | collective-permute-start | bytes 835592 | tf_op jit(solution)/shard_map/ppermute | solution.py:24

commit v2 on v1

--- a/solution.py
+++ b/solution.py
@@ -95,6 +95,12 @@
     return value.reshape((count,) + rest), rider
 
 
+def gather_small(value, axis):
+    count = lax.axis_size(axis)
+    spread = jnp.broadcast_to(value[None], (count,) + value.shape)
+    return lax.all_to_all(spread, axis, 0, 0)
+
+
 def layer(feats, hub_feats, hub_ids, tile_src, tile_mask, w_stack, cotangent):
     rows, width = feats.shape
     tile = tile_mask.shape[1]
@@ -108,15 +114,15 @@
     up = list(range(log2(regions)))
     down = up[::-1]
     prev = shifted(feats[rows - tile :], "dom", 1)
-    hub_table = gather_ordered(hub_feats, "region", down)[0].reshape(total_hubs, width)
+    hub_table = gather_small(hub_feats, "region").reshape(total_hubs, width)
     window = jnp.concatenate([prev, feats], axis=0)
     src = tile_src.reshape(nblk, per_block)
     chosen = src[:, :, None] == lax.broadcasted_iota(jnp.int32, (nblk, per_block, nblk + 1), 2)
     masks = tile_mask.reshape(nblk, per_block, tile, 1, tile)
     links = jnp.where(chosen[:, :, None, :, None], masks, 0).sum(axis=1)
     links = links.reshape(rows, (nblk + 1) * tile)
+    cnt = links.sum(axis=1)
     nsum = jnp.dot(links.astype(jnp.bfloat16), window, preferred_element_type=jnp.float32)
-    cnt = tile_mask.reshape(nblk, per_block, tile, tile).sum(axis=(1, 3)).reshape(rows)
     deg = 1.0 + cnt.astype(jnp.float32) + jnp.float32(hub_count)
     hub_cols = lax.broadcasted_iota(jnp.int32, (rows, total_hubs), 1)
     counts = jnp.zeros((rows, total_hubs), jnp.float32)
@@ -126,8 +132,7 @@
     hsum = jnp.dot(counts, hub_table, preferred_element_type=jnp.float32)
     agg = ((feats.astype(jnp.float32) + nsum + hsum) / deg[:, None]).astype(jnp.bfloat16)
     inputs = jnp.concatenate([feats, agg], axis=1)
-    z_self = jnp.dot(feats, w_stack[:width], preferred_element_type=jnp.float32)
-    z = z_self + jnp.dot(agg, w_stack[width:], preferred_element_type=jnp.float32)
+    z = jnp.dot(inputs, w_stack, preferred_element_type=jnp.float32)
     sig = jax.nn.sigmoid(z)
     activ = (z * sig).astype(jnp.bfloat16)
     dz = (cotangent.astype(jnp.float32) * sig * (1.0 + z * (1.0 - sig))).astype(jnp.bfloat16)

time: 65 us -> 63.1 us (0.971)
  waiting for transfers between devices: 29.9 us -> 21.8 us
  starting transfers between devices: 16.7 us -> 21.7 us
  local copies, waits for them, and re-layouts: 3.49 us -> 6.94 us
  matrix products: 9.53 us -> 6.08 us
  other arithmetic: 3.9 us -> 5.08 us
    all_to_all x0 -> x1, starting transfers between devices: none -> 5.2 us  [gather_small(): return lax.all_to_all(spread, axis, 0, 0)]
    ppermute x6, waiting for transfers between devices: 20.9 us -> 16.6 us  [exchange(): flat = lax.ppermute(flat, axis, pairs).astype(kind)]
    ppermute x5 -> x2, waiting for transfers between devices: 9.07 us -> 5.16 us  [gather_ordered(): got = lax.ppermute(value, axis, pairs)]
    ppermute x6, starting transfers between devices: 5.72 us -> 8.82 us  [exchange(): flat = lax.ppermute(flat, axis, pairs).astype(kind)]
    ppermute x5 -> x2, starting transfers between devices: 6.81 us -> 4.21 us  [gather_ordered(): got = lax.ppermute(value, axis, pairs)]
    dot_general x2 -> x1, matrix products: 4.29 us -> 1.9 us  [layer(): z = jnp.dot(inputs, w_stack, preferred_element_type=jnp.float32)]
    broadcast_in_dim x0 -> x1, local copies, waits for them, and re-layouts: none -> 1.39 us  [gather_small(): spread = jnp.broadcast_to(value[None], (count,) + value.shape)]
    reduce_sum x3 -> x1, other arithmetic: 0.87 us -> 2.09 us  [layer(): cnt = links.sum(axis=1)]
  transfers between devices with their start and end apart: 12 -> 10, of which waited for: 9 -> 8; matrix products, arithmetic and copies ran while one was open for 14% -> 14% of each run, Pallas kernels for 0% -> 0%
where the time goes in v2:
time: 63.1 us; the launch traced here: 62.7 us
  waiting for transfers between devices  21.8 us (35%)
  starting transfers between devices  21.7 us (34%)
  local copies, waits for them, and re-layouts  6.94 us (11%)
  matrix products  6.08 us (10%)
  other arithmetic  5.08 us (8%)
  between operations  1.04 us (2%)
    ppermute x6, waiting for transfers between devices, exchange(): flat = lax.ppermute(flat, axis, pairs).astype(kind)  16.6 us
    ppermute x6, starting transfers between devices, exchange(): flat = lax.ppermute(flat, axis, pairs).astype(kind)  8.82 us
    all_to_all x1, starting transfers between devices, gather_small(): return lax.all_to_all(spread, axis, 0, 0)  5.2 us
    ppermute x2, waiting for transfers between devices, gather_ordered(): got = lax.ppermute(value, axis, pairs)  5.16 us
    ppermute x2, starting transfers between devices, gather_ordered(): got = lax.ppermute(value, axis, pairs)  4.21 us
    ppermute x1, starting transfers between devices, shifted(): lax.ppermute(value, axis, [(source, source + steps) for source in range(i...  3.49 us
    reduce_sum x1, other arithmetic, layer(): cnt = links.sum(axis=1)  2.09 us
    dot_general x1, matrix products, layer(): z = jnp.dot(inputs, w_stack, preferred_element_type=jnp.float32)  1.9 us
  transfers between devices with their start and end apart: 10, of which 8 were waited for; matrix products, arithmetic and copies ran while one was open for 14% of the time, Pallas kernels for 0%

profile of v2, /device:TPU:0, one launch (start us, length us, event | category | flops | bytes accessed | tf_op | source)
XLA Modules:
  0.0 62.7 jit_solution(13385963790238502481)
XLA Ops:
  0.6 0.0 copy-start
  0.6 1.4 %broadcast_in_dim.35 = bf16[8,8,512]{2,1,0:T(8,128)(2,1)} broadcast(bf16[8,512]{1,0:T(8,128)(2,1)} %param.8), dimensions={1,2} | broadcast | bytes 73728 | tf_op jit(solution)/shard_map/broadcast_in_dim | solution.py:100
  2.0 5.2 %all-to-all-start = ((bf16[8,8,512]{2,1,0:T(8,128)(2,1)}), bf16[8,8,512]{2,1,0:T(8,128)(2,1)S(1)}, u32[]{:S(2)}, u32[]{:S(2)}) async-start(bf16[8,8,512]{2,1,0:T(8,128)(2,1)} %broadcast_in_dim.35), calls=%async_computation | async-start | bytes 131072 | tf_op jit(solution)/shard_map/all_to_all | solution.py:101
  7.2 0.9 %slice.48 = bf16[128,512]{1,0:T(8,128)(2,1)S(1)} slice(bf16[512,512]{1,0:T(8,128)(2,1)} %param.7), slice={[384:512], [0:512]} | slice | bytes 262144 | tf_op jit(solution)/shard_map/slice | solution.py:116
  8.1 3.5 %collective-permute-start = (bf16[128,512]{1,0:T(8,128)(2,1)S(1)}, bf16[128,512]{1,0:T(8,128)(2,1)S(1)}, u32[]{:S(2)}, u32[]{:S(2)}) collective-permute-start(bf16[128,512]{1,0:T(8,128)(2,1)S(1)} %slice.48), channel_id=1, source_target_pairs={{0,1},{1,2},{2,3},{4,5},{5,6},{6,7},{8,9},{9,10},{10,11},{12,13},{... | collective-permute-start | bytes 393224 | tf_op jit(solution)/shard_map/ppermute | solution.py:10
  11.6 0.9 %fusion.32 = (s32[512,1]{0,1:T(1,128)S(1)}, s32[512,1]{0,1:T(1,128)S(1)}, s32[512,1]{0,1:T(1,128)S(1)}, s32[512,1]{0,1:T(1,128)S(1)}) fusion(s32[512,4]{0,1:T(4,128)} %param.9), kind=kLoop, calls=%fused_computation.85 | loop fusion | bytes 16384 | tf_op jit(solution)/shard_map/slice | solution.py:130
  12.5 0.7 %eq.69 = s32[4,4]{1,0:T(4,128)S(1)} reshape(s32[16]{0:T(128)} %param.10) | data formatting | bytes 128 | tf_op jit(solution)/shard_map/eq | solution.py:120
  13.2 0.1 iota_compare_fusion.4
  13.3 2.1 %select_reduce_fusion = (s32[4,128]{1,0:T(4,128)S(1)}, s32[4,128,5,128]{3,1,2,0:T(8,128)S(1)}) fusion(s32[4,4,128,128]{3,2,1,0:T(8,128)} %bitcast.110, pred[4,4,5]{2,1,0:T(4,128)(4,1)S(1)} %iota_compare_fusion.4), kind=kLoop, calls=%fused_computation | loop fusion | flops 3603968 | bytes 2361424 | tf_op jit(solution)/shard_map/reduce_sum | solution.py:124
  15.4 0.0 copy-done
  15.4 0.2 copy.30
  15.7 0.1 convert_element_type.56
  15.8 0.9 %copy.29 = bf16[4,128,5,128]{1,0,3,2:T(4,128)(2,1)S(1)} copy(bf16[4,128,5,128]{3,1,2,0:T(8,128)(2,1)S(1)} %convert_element_type.56) | data formatting | bytes 1310720 | tf_op jit(solution)/shard_map/convert_element_type | solution.py:125
  16.7 0.0 all-to-all-done
  16.7 0.9 %fusion.19 = f32[512,512]{0,1:T(8,128)S(1)} fusion(s32[512]{0:T(512)S(1)} %bitcast.126, s32[512]{0:T(512)S(1)} %bitcast.128, s32[512]{0:T(512)S(1)} %bitcast.124, s32[512]{0:T(512)S(1)} %bitcast.122, bf16[8,8,512]{2,1,0:T(8,128)(2,1)S(1)} %all-to-all-done), kind=kOutput, calls=%fused_computation.46 | convolution fusion | flops 33947648 | bytes 1122304 | tf_op jit(solution)/shard_map/dot_general | solution.py:132
  17.7 0.0 collective-permute-done
  17.7 0.0 copy-start.2
  17.7 0.0 copy-start.3
  17.7 0.7 %fusion.2 = bf16[512,512]{0,1:T(8,128)(2,1)S(1)} fusion(f32[512,512]{0,1:T(8,128)S(1)} %fusion.19, bf16[512,512]{0,1:T(8,128)(2,1)S(1)} %copy.30, bf16[80,8,4,128]{3,2,1,0:T(4,128)(2,1)S(1)} %bitcast.113, bf16[512,512]{1,0:T(8,128)(2,1)S(1)} %copy-done, bf16[128,512]{1,0:T(8,128)(2,1)S(1)} %collective-permute-done, f32[512]{0:T(512)S(1)} %add_bitcast_fusion), kind=kOutput, calls=%fused_computation.6 | convolution fusion | flops 338165760 | bytes 3409920 | tf_op jit(solution)/shard_map/dot_general | solution.py:125
  18.4 0.5 copy-done.2
  18.9 0.1 copy-done.3
  19.1 1.9 %multiply_convert_fusion = (bf16[512,512]{1,0:T(8,128)(2,1)S(1)}, bf16[512,512]{1,0:T(8,128)(2,1)}) fusion(bf16[512,512]{1,0:T(8,128)(2,1)S(1)} %copy-done.3, bf16[1024,512]{1,0:T(8,128)(2,1)S(1)} %copy-done.2, bf16[512,512]{0,1:T(8,128)(2,1)S(1)} %fusion.2, bf16[512,512]{0,1:T(8,128)(2,1)S(1)} %copy.30), kind=kOutput, calls=%fused_computation.11 | convolution fusion | flops 542113792 | bytes 3670016 | tf_op jit(solution)/shard_map/dot_general | solution.py:135
  21.0 0.0 copy-start.1
  21.0 0.7 %fusion.5 = f32[1024,512]{1,0:T(8,128)S(1)} fusion(bf16[512,512]{1,0:T(8,128)(2,1)S(1)} %get-tuple-element.5, bf16[512,512]{0,1:T(8,128)(2,1)S(1)} %fusion.2, bf16[512,512]{0,1:T(8,128)(2,1)S(1)} %copy.30), kind=kOutput, calls=%fused_computation.14 | convolution fusion | flops 538968064 | bytes 3670016 | tf_op jit(solution)/shard_map/dot_general | solution.py:139
  21.7 0.1 constant_dynamic-slice_fusion.5
  21.8 0.0 copy-done.1
  21.8 0.3 collective-permute-start.1
  22.1 1.9 %fusion.4 = f32[64,512]{1,0:T(8,128)S(1)} fusion(bf16[512,512]{1,0:T(8,128)(2,1)} %copy-done.1, bf16[1024,512]{1,0:T(8,128)(2,1)} %param.12, f32[512]{0:T(512)S(1)} %add_bitcast_fusion, s32[512]{0:T(512)S(1)} %bitcast.127, s32[512]{0:T(512)S(1)} %bitcast.129, s32[512]{0:T(512)S(1)} %bitcast.125, s32[512]{0:T(512)S(1)} %bitcast.123), kind=kOutput, calls=%fused_computation.8 | convolution fusion | flops 302907392 | bytes 1189888 | tf_op jit(solution)/shard_map/dot_general | solution.py:146
  24.0 0.6 collective-permute-done.1
  24.6 1.4 %bitcast_add_fusion = f32[4,2,2,32,512]{4,3,2,1,0:T(8,128)S(1)} fusion(f32[4,2,2,32,512]{4,3,2,1,0:T(8,128)} %bitcast.10, f32[4,2,2,2,32,512]{5,4,3,2,1,0:T(8,128)S(1)} %bitcast.105, s32[]{:T(128)S(6)} %select_n.188), kind=kLoop, calls=%fused_computation.10 | loop fusion | flops 262144 | bytes 3145732 | tf_op jit(solution)/shard_map/add | solution.py:67
  26.2 0.1 fusion.12
  26.3 2.1 %collective-permute-start.2 = (bf16[288,512]{1,0:T(8,128)(2,1)S(1)}, bf16[288,512]{1,0:T(8,128)(2,1)S(1)}, u32[]{:S(2)}, u32[]{:S(2)}) collective-permute-start(bf16[288,512]{1,0:T(8,128)(2,1)S(1)} %pad_maximum_fusion.4), channel_id=1, source_target_pairs={{0,8},{4,20},{8,0},{12,28},{16,24},{20,4},{24,16},{28,12},{1,9},{5... | collective-permute-start | bytes 884744 | tf_op jit(solution)/shard_map/ppermute | solution.py:24
  28.4 4.7 %collective-permute-done.2 = bf16[288,512]{1,0:T(8,128)(2,1)S(1)} collective-permute-done((bf16[288,512]{1,0:T(8,128)(2,1)S(1)}, bf16[288,512]{1,0:T(8,128)(2,1)S(1)}, u32[]{:S(2)}, u32[]{:S(2)}) %collective-permute-start.2) | collective-permute-done | bytes 294944 | tf_op jit(solution)/shard_map/ppermute | solution.py:24
  33.1 0.1 slice.64
  33.2 0.2 fusion.13
  33.4 2.1 %collective-permute-start.3 = (bf16[144,512]{1,0:T(8,128)(2,1)S(1)}, bf16[144,512]{1,0:T(8,128)(2,1)S(1)}, u32[]{:S(2)}, u32[]{:S(2)}) collective-permute-start(bf16[144,512]{1,0:T(8,128)(2,1)S(1)} %pad_maximum_fusion.9), channel_id=1, source_target_pairs={{0,16},{4,12},{8,24},{12,4},{16,0},{20,28},{24,8},{28,20},{1,17},{... | collective-permute-start | bytes 442376 | tf_op jit(solution)/shard_map/ppermute | solution.py:24
  35.5 3.1 %collective-permute-done.3 = bf16[144,512]{1,0:T(8,128)(2,1)S(1)} collective-permute-done((bf16[144,512]{1,0:T(8,128)(2,1)S(1)}, bf16[144,512]{1,0:T(8,128)(2,1)S(1)}, u32[]{:S(2)}, u32[]{:S(2)}) %collective-permute-start.3) | collective-permute-done | bytes 147488 | tf_op jit(solution)/shard_map/ppermute | solution.py:24
  38.8 1.6 %collective-permute-start.4 = (f32[80,512]{1,0:T(8,128)S(1)}, f32[80,512]{1,0:T(8,128)S(1)}, u32[]{:S(2)}, u32[]{:S(2)}) collective-permute-start(f32[80,512]{1,0:T(8,128)S(1)} %pad_maximum_fusion.8), channel_id=1, source_target_pairs={{0,1},{1,0},{2,3},{3,2},{4,5},{5,4},{6,7},{7,6},{8,9},{9,8},{10,11... | collective-permute-start | bytes 491528 | tf_op jit(solution)/shard_map/ppermute | solution.py:24
  40.4 3.7 %collective-permute-done.4 = f32[80,512]{1,0:T(8,128)S(1)} collective-permute-done((f32[80,512]{1,0:T(8,128)S(1)}, f32[80,512]{1,0:T(8,128)S(1)}, u32[]{:S(2)}, u32[]{:S(2)}) %collective-permute-start.4) | collective-permute-done | bytes 163872 | tf_op jit(solution)/shard_map/ppermute | solution.py:24
  44.3 2.6 %collective-permute-start.5 = (f32[48,512]{1,0:T(8,128)S(1)}, f32[48,512]{1,0:T(8,128)S(1)}, u32[]{:S(2)}, u32[]{:S(2)}) collective-permute-start(f32[48,512]{1,0:T(8,128)S(1)} %pad_maximum_fusion.11), channel_id=1, source_target_pairs={{0,2},{1,3},{2,0},{3,1},{4,6},{5,7},{6,4},{7,5},{8,10},{9,11},{10,... | collective-permute-start | bytes 294920 | tf_op jit(solution)/shard_map/ppermute | solution.py:24
  46.9 2.9 %collective-permute-done.5 = f32[48,512]{1,0:T(8,128)S(1)} collective-permute-done((f32[48,512]{1,0:T(8,128)S(1)}, f32[48,512]{1,0:T(8,128)S(1)}, u32[]{:S(2)}, u32[]{:S(2)}) %collective-permute-start.5) | collective-permute-done | bytes 98336 | tf_op jit(solution)/shard_map/ppermute | solution.py:24
  49.9 2.1 %collective-permute-start.6 = (f32[32,512]{1,0:T(8,128)S(1)}, f32[32,512]{1,0:T(8,128)S(1)}, u32[]{:S(2)}, u32[]{:S(2)}) collective-permute-start(f32[32,512]{1,0:T(8,128)S(1)} %slice_add_fusion), channel_id=1, source_target_pairs={{0,16},{4,20},{8,24},{12,28},{16,0},{20,4},{24,8},{28,12},{1,17},{... | collective-permute-start | bytes 196616 | tf_op jit(solution)/shard_map/ppermute | solution.py:87
  52.0 2.2 %collective-permute-done.6 = f32[32,512]{1,0:T(8,128)S(1)} collective-permute-done((f32[32,512]{1,0:T(8,128)S(1)}, f32[32,512]{1,0:T(8,128)S(1)}, u32[]{:S(2)}, u32[]{:S(2)}) %collective-permute-start.6) | collective-permute-done | bytes 65568 | tf_op jit(solution)/shard_map/ppermute | solution.py:87
  54.3 2.1 %collective-permute-start.7 = (f32[2,32,512]{2,1,0:T(8,128)S(1)}, f32[2,32,512]{2,1,0:T(8,128)S(1)}, u32[]{:S(2)}, u32[]{:S(2)}) collective-permute-start(f32[2,32,512]{2,1,0:T(8,128)S(1)} %pad_maximum_fusion.10), channel_id=1, source_target_pairs={{0,8},{4,12},{8,0},{12,4},{16,24},{20,28},{24,16},{28,20},{1,9},{5... | collective-permute-start | bytes 393224 | tf_op jit(solution)/shard_map/ppermute | solution.py:87
  56.4 2.9 %collective-permute-done.7 = f32[2,32,512]{2,1,0:T(8,128)S(1)} collective-permute-done((f32[2,32,512]{2,1,0:T(8,128)S(1)}, f32[2,32,512]{2,1,0:T(8,128)S(1)}, u32[]{:S(2)}, u32[]{:S(2)}) %collective-permute-start.7) | collective-permute-done | bytes 131104 | tf_op jit(solution)/shard_map/ppermute | solution.py:87
  59.5 0.1 collective-permute-start.8
  59.5 1.5 %collective-permute-done.8 = f32[136,512]{1,0:T(8,128)S(1)} collective-permute-done((f32[136,512]{1,0:T(8,128)S(1)}, f32[136,512]{1,0:T(8,128)S(1)}, u32[]{:S(2)}, u32[]{:S(2)}) %collective-permute-start.8) | collective-permute-done | bytes 278560 | tf_op jit(solution)/shard_map/ppermute | solution.py:24
  61.2 0.8 %copy.34 = f32[2,2,2,32,512]{4,3,2,1,0:T(8,128)} copy(f32[2,2,2,32,512]{4,3,1,0,2:T(8,128)S(1)} %pad_maximum_fusion.3) | data formatting | bytes 1048576 | tf_op jit(solution)/shard_map/stack | solution.py:90
  62.0 0.6 slice_add_fusion.2
  (36 shorter events, 0.7 us)
Async XLA Ops:
  0.6 14.8 %copy-start = (bf16[512,512]{1,0:T(8,128)(2,1)S(1)}, bf16[512,512]{1,0:T(8,128)(2,1)}, u32[]{:S(2)}) copy-start(bf16[512,512]{1,0:T(8,128)(2,1)} %param.7) | copy-start | bytes 1572868
  2.0 14.7 %all-to-all-start = ((bf16[8,8,512]{2,1,0:T(8,128)(2,1)}), bf16[8,8,512]{2,1,0:T(8,128)(2,1)S(1)}, u32[]{:S(2)}, u32[]{:S(2)}) async-start(bf16[8,8,512]{2,1,0:T(8,128)(2,1)} %broadcast_in_dim.35), calls=%async_computation | async-start | bytes 131072 | tf_op jit(solution)/shard_map/all_to_all | solution.py:101
  8.1 9.6 %collective-permute-start = (bf16[128,512]{1,0:T(8,128)(2,1)S(1)}, bf16[128,512]{1,0:T(8,128)(2,1)S(1)}, u32[]{:S(2)}, u32[]{:S(2)}) collective-permute-start(bf16[128,512]{1,0:T(8,128)(2,1)S(1)} %slice.48), channel_id=1, source_target_pairs={{0,1},{1,2},{2,3},{4,5},{5,6},{6,7},{8,9},{9,10},{10,11},{12,13},{... | collective-permute-start | bytes 393224 | tf_op jit(solution)/shard_map/ppermute | solution.py:10
  17.7 1.2 %copy-start.2 = (bf16[1024,512]{1,0:T(8,128)(2,1)S(1)}, bf16[1024,512]{1,0:T(8,128)(2,1)}, u32[]{:S(2)}) copy-start(bf16[1024,512]{1,0:T(8,128)(2,1)} %param.12) | copy-start | bytes 3145732
  17.7 1.3 %copy-start.3 = (bf16[512,512]{1,0:T(8,128)(2,1)S(1)}, bf16[512,512]{1,0:T(8,128)(2,1)}, u32[]{:S(2)}) copy-start(bf16[512,512]{1,0:T(8,128)(2,1)} %param.13) | copy-start | bytes 1572868
  21.0 0.8 %copy-start.1 = (bf16[512,512]{1,0:T(8,128)(2,1)}, bf16[512,512]{1,0:T(8,128)(2,1)S(1)}, u32[]{:S(2)}) copy-start(bf16[512,512]{1,0:T(8,128)(2,1)S(1)} %get-tuple-element.5) | copy-start | bytes 1572868
  21.8 2.9 %collective-permute-start.1 = (f32[512,512]{1,0:T(8,128)S(1)}, f32[512,512]{1,0:T(8,128)}, u32[]{:S(2)}, u32[]{:S(2)}) collective-permute-start(f32[512,512]{1,0:T(8,128)S(1)} %bitcast.107), channel_id=1, source_target_pairs={{0,4},{4,0},{8,12},{12,8},{16,20},{20,16},{24,28},{28,24},{1,5},{5... | collective-permute-start | bytes 3145736 | tf_op jit(solution)/shard_map/ppermute | solution.py:24
  26.3 6.8 %collective-permute-start.2 = (bf16[288,512]{1,0:T(8,128)(2,1)S(1)}, bf16[288,512]{1,0:T(8,128)(2,1)S(1)}, u32[]{:S(2)}, u32[]{:S(2)}) collective-permute-start(bf16[288,512]{1,0:T(8,128)(2,1)S(1)} %pad_maximum_fusion.4), channel_id=1, source_target_pairs={{0,8},{4,20},{8,0},{12,28},{16,24},{20,4},{24,16},{28,12},{1,9},{5... | collective-permute-start | bytes 884744 | tf_op jit(solution)/shard_map/ppermute | solution.py:24
  33.4 5.2 %collective-permute-start.3 = (bf16[144,512]{1,0:T(8,128)(2,1)S(1)}, bf16[144,512]{1,0:T(8,128)(2,1)S(1)}, u32[]{:S(2)}, u32[]{:S(2)}) collective-permute-start(bf16[144,512]{1,0:T(8,128)(2,1)S(1)} %pad_maximum_fusion.9), channel_id=1, source_target_pairs={{0,16},{4,12},{8,24},{12,4},{16,0},{20,28},{24,8},{28,20},{1,17},{... | collective-permute-start | bytes 442376 | tf_op jit(solution)/shard_map/ppermute | solution.py:24
  38.8 5.4 %collective-permute-start.4 = (f32[80,512]{1,0:T(8,128)S(1)}, f32[80,512]{1,0:T(8,128)S(1)}, u32[]{:S(2)}, u32[]{:S(2)}) collective-permute-start(f32[80,512]{1,0:T(8,128)S(1)} %pad_maximum_fusion.8), channel_id=1, source_target_pairs={{0,1},{1,0},{2,3},{3,2},{4,5},{5,4},{6,7},{7,6},{8,9},{9,8},{10,11... | collective-permute-start | bytes 491528 | tf_op jit(solution)/shard_map/ppermute | solution.py:24
  44.3 5.6 %collective-permute-start.5 = (f32[48,512]{1,0:T(8,128)S(1)}, f32[48,512]{1,0:T(8,128)S(1)}, u32[]{:S(2)}, u32[]{:S(2)}) collective-permute-start(f32[48,512]{1,0:T(8,128)S(1)} %pad_maximum_fusion.11), channel_id=1, source_target_pairs={{0,2},{1,3},{2,0},{3,1},{4,6},{5,7},{6,4},{7,5},{8,10},{9,11},{10,... | collective-permute-start | bytes 294920 | tf_op jit(solution)/shard_map/ppermute | solution.py:24
  49.9 4.4 %collective-permute-start.6 = (f32[32,512]{1,0:T(8,128)S(1)}, f32[32,512]{1,0:T(8,128)S(1)}, u32[]{:S(2)}, u32[]{:S(2)}) collective-permute-start(f32[32,512]{1,0:T(8,128)S(1)} %slice_add_fusion), channel_id=1, source_target_pairs={{0,16},{4,20},{8,24},{12,28},{16,0},{20,4},{24,8},{28,12},{1,17},{... | collective-permute-start | bytes 196616 | tf_op jit(solution)/shard_map/ppermute | solution.py:87
  54.3 5.0 %collective-permute-start.7 = (f32[2,32,512]{2,1,0:T(8,128)S(1)}, f32[2,32,512]{2,1,0:T(8,128)S(1)}, u32[]{:S(2)}, u32[]{:S(2)}) collective-permute-start(f32[2,32,512]{2,1,0:T(8,128)S(1)} %pad_maximum_fusion.10), channel_id=1, source_target_pairs={{0,8},{4,12},{8,0},{12,4},{16,24},{20,28},{24,16},{28,20},{1,9},{5... | collective-permute-start | bytes 393224 | tf_op jit(solution)/shard_map/ppermute | solution.py:87
  59.5 1.6 %collective-permute-start.8 = (f32[136,512]{1,0:T(8,128)S(1)}, f32[136,512]{1,0:T(8,128)S(1)}, u32[]{:S(2)}, u32[]{:S(2)}) collective-permute-start(f32[136,512]{1,0:T(8,128)S(1)} %pad_maximum_fusion.5), channel_id=1, source_target_pairs={{0,4},{4,0},{8,12},{12,8},{16,20},{20,16},{24,28},{28,24},{1,5},{5... | collective-permute-start | bytes 835592 | tf_op jit(solution)/shard_map/ppermute | solution.py:24

commit v3 on v1

--- a/solution.py
+++ b/solution.py
@@ -107,7 +107,7 @@
     total_hubs = owned * regions
     up = list(range(log2(regions)))
     down = up[::-1]
-    prev = shifted(feats[rows - tile :], "dom", 1)
+    prev = shifted(feats, "dom", 1)[rows - tile :]
     hub_table = gather_ordered(hub_feats, "region", down)[0].reshape(total_hubs, width)
     window = jnp.concatenate([prev, feats], axis=0)
     src = tile_src.reshape(nblk, per_block)
@@ -126,8 +126,7 @@
     hsum = jnp.dot(counts, hub_table, preferred_element_type=jnp.float32)
     agg = ((feats.astype(jnp.float32) + nsum + hsum) / deg[:, None]).astype(jnp.bfloat16)
     inputs = jnp.concatenate([feats, agg], axis=1)
-    z_self = jnp.dot(feats, w_stack[:width], preferred_element_type=jnp.float32)
-    z = z_self + jnp.dot(agg, w_stack[width:], preferred_element_type=jnp.float32)
+    z = jnp.dot(inputs, w_stack, preferred_element_type=jnp.float32)
     sig = jax.nn.sigmoid(z)
     activ = (z * sig).astype(jnp.bfloat16)
     dz = (cotangent.astype(jnp.float32) * sig * (1.0 + z * (1.0 - sig))).astype(jnp.bfloat16)

time: 65 us -> 65.5 us (level)
  matrix products: 9.53 us -> 6.09 us
  starting transfers between devices: 16.7 us -> 19.7 us
  waiting for transfers between devices: 29.9 us -> 28.3 us
  other arithmetic: 3.9 us -> 5.27 us
  local copies, waits for them, and re-layouts: 3.49 us -> 4.71 us
    ppermute x6, waiting for transfers between devices: 20.9 us -> 18 us  [exchange(): flat = lax.ppermute(flat, axis, pairs).astype(kind)]
    ppermute x6, starting transfers between devices: 5.72 us -> 8.42 us  [exchange(): flat = lax.ppermute(flat, axis, pairs).astype(kind)]
    dot_general x2 -> x1, matrix products: 4.29 us -> 1.9 us  [layer(): z = jnp.dot(inputs, w_stack, preferred_element_type=jnp.float32)]
    ppermute x1, waiting for transfers between devices: 0.01 us -> 1.42 us  [shifted(): lax.ppermute(value, axis, [(source, source + steps) for source in range(i...]
    reduce_sum x1, other arithmetic: 0.51 us -> 1.88 us  [layer(): links = jnp.where(chosen[:, :, None, :, None], masks, 0).sum(axis=1)]
    dot_general x1, matrix products: 1.72 us -> 0.66 us  [layer(): jnp.dot(links.astype(jnp.bfloat16), window, preferred_element_type=jnp.fl...]
  transfers between devices with their start and end apart: 12 -> 12, of which waited for: 9 -> 10; matrix products, arithmetic and copies ran while one was open for 14% -> 11% of each run, Pallas kernels for 0% -> 0%
where the time goes in v3:
time: 65.5 us; the launch traced here: 65.2 us
  waiting for transfers between devices  28.3 us (43%)
  starting transfers between devices  19.7 us (30%)
  matrix products  6.09 us (9%)
  other arithmetic  5.27 us (8%)
  local copies, waits for them, and re-layouts  4.71 us (7%)
  between operations  1.17 us (2%)
    ppermute x6, waiting for transfers between devices, exchange(): flat = lax.ppermute(flat, axis, pairs).astype(kind)  18 us
    ppermute x5, waiting for transfers between devices, gather_ordered(): got = lax.ppermute(value, axis, pairs)  8.91 us
    ppermute x6, starting transfers between devices, exchange(): flat = lax.ppermute(flat, axis, pairs).astype(kind)  8.42 us
    ppermute x5, starting transfers between devices, gather_ordered(): got = lax.ppermute(value, axis, pairs)  6.95 us
    ppermute x1, starting transfers between devices, shifted(): lax.ppermute(value, axis, [(source, source + steps) for source in range(i...  4.28 us
    dot_general x1, matrix products, layer(): z = jnp.dot(inputs, w_stack, preferred_element_type=jnp.float32)  1.9 us
    dot_general x1, matrix products, layer(): lax.dot_general(counts, sgrad, (((0,), (0,)), ((), ())), preferred_elemen...  1.88 us
    reduce_sum x1, other arithmetic, layer(): links = jnp.where(chosen[:, :, None, :, None], masks, 0).sum(axis=1)  1.88 us
  transfers between devices with their start and end apart: 12, of which 10 were waited for; matrix products, arithmetic and copies ran while one was open for 11% of the time, Pallas kernels for 0%

profile of v3, /device:TPU:0, one launch (start us, length us, event | category | flops | bytes accessed | tf_op | source)
XLA Modules:
  0.0 65.2 jit_solution(11529093064271014067)
XLA Ops:
  0.6 0.0 copy-start.4
  0.6 0.0 copy-start.2
  0.7 0.0 copy-start
  0.7 0.0 copy-start.3
  0.7 3.1 %collective-permute-start.1 = (bf16[8,512]{1,0:T(8,128)(2,1)}, bf16[8,512]{1,0:T(8,128)(2,1)S(1)}, u32[]{:S(2)}, u32[]{:S(2)}) collective-permute-start(bf16[8,512]{1,0:T(8,128)(2,1)} %param.8), channel_id=1, source_target_pairs={{0,16},{4,20},{8,24},{12,28},{16,0},{20,4},{24,8},{28,12},{1,17},{... | collective-permute-start | bytes 24584 | tf_op jit(solution)/shard_map/ppermute | solution.py:87
  3.7 4.3 %collective-permute-start = (bf16[512,512]{1,0:T(8,128)(2,1)}, bf16[512,512]{1,0:T(8,128)(2,1)}, u32[]{:S(2)}, u32[]{:S(2)}) collective-permute-start(bf16[512,512]{1,0:T(8,128)(2,1)} %param.7), channel_id=1, source_target_pairs={{0,1},{1,2},{2,3},{4,5},{5,6},{6,7},{8,9},{9,10},{10,11},{12,13},{... | collective-permute-start | bytes 1572872 | tf_op jit(solution)/shard_map/ppermute | solution.py:10
  8.0 0.7 %eq.75 = s32[4,4]{1,0:T(4,128)S(1)} reshape(s32[16]{0:T(128)} %param.10) | data formatting | bytes 128 | tf_op jit(solution)/shard_map/eq | solution.py:114
  8.8 0.1 iota_compare_fusion.4
  8.8 1.9 %select_reduce_fusion = s32[4,128,5,128]{3,1,2,0:T(8,128)S(1)} fusion(s32[4,4,128,128]{3,2,1,0:T(8,128)} %bitcast.122, pred[4,4,5]{2,1,0:T(4,128)(4,1)S(1)} %iota_compare_fusion.4), kind=kLoop, calls=%fused_computation | loop fusion | flops 2293760 | bytes 2359376 | tf_op jit(solution)/shard_map/reduce_sum | solution.py:116
  10.7 0.0 collective-permute-done.1
  10.7 0.0 copy-done.4
  10.8 1.6 %collective-permute-start.2 = (bf16[2,8,512]{2,1,0:T(8,128)(2,1)S(1)}, bf16[2,8,512]{2,1,0:T(8,128)(2,1)S(1)}, u32[]{:S(2)}, u32[]{:S(2)}) collective-permute-start(bf16[2,8,512]{2,1,0:T(8,128)(2,1)S(1)} %pad_maximum_fusion.14), channel_id=1, source_target_pairs={{0,8},{4,12},{8,0},{12,4},{16,24},{20,28},{24,16},{28,20},{1,9},{5... | collective-permute-start | bytes 49160 | tf_op jit(solution)/shard_map/ppermute | solution.py:87
  12.3 0.0 copy-done.3
  12.3 0.0 copy-done
  12.4 0.3 reduce_sum.26
  12.7 1.8 %collective-permute-done.2 = bf16[2,8,512]{2,1,0:T(8,128)(2,1)S(1)} collective-permute-done((bf16[2,8,512]{2,1,0:T(8,128)(2,1)S(1)}, bf16[2,8,512]{2,1,0:T(8,128)(2,1)S(1)}, u32[]{:S(2)}, u32[]{:S(2)}) %collective-permute-start.2) | collective-permute-done | bytes 16416 | tf_op jit(solution)/shard_map/ppermute | solution.py:87
  14.6 0.1 collective-permute-start.3
  14.7 0.0 copy-done.2
  14.7 0.2 copy.36
  14.9 0.1 convert_element_type.56
  15.1 0.9 %copy.33 = bf16[4,128,5,128]{1,0,3,2:T(4,128)(2,1)S(1)} copy(bf16[4,128,5,128]{3,1,2,0:T(8,128)(2,1)S(1)} %convert_element_type.56) | data formatting | bytes 1310720 | tf_op jit(solution)/shard_map/convert_element_type | solution.py:118
  16.0 0.0 collective-permute-done.3
  16.0 0.9 %fusion.19 = f32[512,512]{0,1:T(8,128)S(1)} fusion(bf16[64,512]{1,0:T(8,128)(2,1)S(1)} %bitcast.137, s32[512]{0:T(512)S(1)} %bitcast.144, s32[512]{0:T(512)S(1)} %bitcast.146, s32[512]{0:T(512)S(1)} %bitcast.142, s32[512]{0:T(512)S(1)} %bitcast.140), kind=kOutput, calls=%fused_computation.45 | convolution fusion | flops 33947648 | bytes 1122304 | tf_op jit(solution)/shard_map/dot_general | solution.py:126
  17.0 1.4 %collective-permute-done = bf16[512,512]{1,0:T(8,128)(2,1)} collective-permute-done((bf16[512,512]{1,0:T(8,128)(2,1)}, bf16[512,512]{1,0:T(8,128)(2,1)}, u32[]{:S(2)}, u32[]{:S(2)}) %collective-permute-start) | collective-permute-done | bytes 524320 | tf_op jit(solution)/shard_map/ppermute | solution.py:10
  18.4 0.9 %slice.64 = bf16[128,512]{1,0:T(8,128)(2,1)S(1)} slice(bf16[512,512]{1,0:T(8,128)(2,1)} %collective-permute-done), slice={[384:512], [0:512]} | slice | bytes 262144 | tf_op jit(solution)/shard_map/slice | solution.py:110
  19.3 0.0 copy-start.5
  19.3 0.0 copy-start.6
  19.4 0.7 %fusion.2 = bf16[512,512]{0,1:T(8,128)(2,1)S(1)} fusion(f32[512,512]{0,1:T(8,128)S(1)} %fusion.19, bf16[512,512]{0,1:T(8,128)(2,1)S(1)} %copy.36, bf16[80,8,4,128]{3,2,1,0:T(4,128)(2,1)S(1)} %bitcast.129, bf16[512,512]{1,0:T(8,128)(2,1)S(1)} %copy-done.2, bf16[128,512]{1,0:T(8,128)(2,1)S(1)} %slice.64, f32[512]{0:T(512)S(1)} %add_bitcast_fusion), kind=kOutput, calls=%fused_computation.5 | convolution fusion | flops 338165760 | bytes 3409920 | tf_op jit(solution)/shard_map/dot_general | solution.py:118
  20.0 0.5 copy-done.5
  20.6 0.1 copy-done.6
  20.7 1.9 %multiply_convert_fusion = (bf16[512,512]{1,0:T(8,128)(2,1)S(1)}, bf16[512,512]{1,0:T(8,128)(2,1)}) fusion(bf16[512,512]{1,0:T(8,128)(2,1)S(1)} %copy-done.6, bf16[1024,512]{1,0:T(8,128)(2,1)S(1)} %copy-done.5, bf16[512,512]{0,1:T(8,128)(2,1)S(1)} %fusion.2, bf16[512,512]{0,1:T(8,128)(2,1)S(1)} %copy.36), kind=kOutput, calls=%fused_computation.10 | convolution fusion | flops 542113792 | bytes 3670016 | tf_op jit(solution)/shard_map/dot_general | solution.py:129
  22.6 0.0 copy-start.1
  22.6 0.7 %fusion.5 = f32[1024,512]{1,0:T(8,128)S(1)} fusion(bf16[512,512]{1,0:T(8,128)(2,1)S(1)} %get-tuple-element.3, bf16[512,512]{0,1:T(8,128)(2,1)S(1)} %fusion.2, bf16[512,512]{0,1:T(8,128)(2,1)S(1)} %copy.36), kind=kOutput, calls=%fused_computation.13 | convolution fusion | flops 538968064 | bytes 3670016 | tf_op jit(solution)/shard_map/dot_general | solution.py:133
  23.3 0.1 constant_dynamic-slice_fusion.5
  23.4 0.0 copy-done.1
  23.4 0.1 collective-permute-start.4
  23.5 1.9 %fusion.4 = f32[64,512]{1,0:T(8,128)S(1)} fusion(bf16[512,512]{1,0:T(8,128)(2,1)} %copy-done.1, bf16[1024,512]{1,0:T(8,128)(2,1)} %param.12, f32[512]{0:T(512)S(1)} %add_bitcast_fusion, s32[512]{0:T(512)S(1)} %bitcast.145, s32[512]{0:T(512)S(1)} %bitcast.147, s32[512]{0:T(512)S(1)} %bitcast.143, s32[512]{0:T(512)S(1)} %bitcast.141), kind=kOutput, calls=%fused_computation.7 | convolution fusion | flops 302907392 | bytes 1189888 | tf_op jit(solution)/shard_map/dot_general | solution.py:140
  25.5 0.8 %collective-permute-done.4 = f32[512,512]{1,0:T(8,128)} collective-permute-done((f32[512,512]{1,0:T(8,128)S(1)}, f32[512,512]{1,0:T(8,128)}, u32[]{:S(2)}, u32[]{:S(2)}) %collective-permute-start.4) | collective-permute-done | bytes 1048608 | tf_op jit(solution)/shard_map/ppermute | solution.py:24
  26.3 1.4 %bitcast_add_fusion = f32[4,2,2,32,512]{4,3,2,1,0:T(8,128)S(1)} fusion(f32[4,2,2,32,512]{4,3,2,1,0:T(8,128)} %bitcast.19, f32[4,2,2,2,32,512]{5,4,3,2,1,0:T(8,128)S(1)} %bitcast.121, s32[]{:T(128)S(6)} %select_n.233), kind=kLoop, calls=%fused_computation.9 | loop fusion | flops 262144 | bytes 3145732 | tf_op jit(solution)/shard_map/add | solution.py:67
  27.8 0.1 fusion.12
  27.9 1.6 %collective-permute-start.5 = (bf16[288,512]{1,0:T(8,128)(2,1)S(1)}, bf16[288,512]{1,0:T(8,128)(2,1)S(1)}, u32[]{:S(2)}, u32[]{:S(2)}) collective-permute-start(bf16[288,512]{1,0:T(8,128)(2,1)S(1)} %pad_maximum_fusion.4), channel_id=1, source_target_pairs={{0,8},{4,20},{8,0},{12,28},{16,24},{20,4},{24,16},{28,12},{1,9},{5... | collective-permute-start | bytes 884744 | tf_op jit(solution)/shard_map/ppermute | solution.py:24
  29.5 5.2 %collective-permute-done.5 = bf16[288,512]{1,0:T(8,128)(2,1)S(1)} collective-permute-done((bf16[288,512]{1,0:T(8,128)(2,1)S(1)}, bf16[288,512]{1,0:T(8,128)(2,1)S(1)}, u32[]{:S(2)}, u32[]{:S(2)}) %collective-permute-start.5) | collective-permute-done | bytes 294944 | tf_op jit(solution)/shard_map/ppermute | solution.py:24
  34.7 0.1 slice.65
  34.8 0.2 fusion.13
  35.0 0.7 %collective-permute-start.6 = (bf16[144,512]{1,0:T(8,128)(2,1)S(1)}, bf16[144,512]{1,0:T(8,128)(2,1)S(1)}, u32[]{:S(2)}, u32[]{:S(2)}) collective-permute-start(bf16[144,512]{1,0:T(8,128)(2,1)S(1)} %pad_maximum_fusion.9), channel_id=1, source_target_pairs={{0,16},{4,12},{8,24},{12,4},{16,0},{20,28},{24,8},{28,20},{1,17},{... | collective-permute-start | bytes 442376 | tf_op jit(solution)/shard_map/ppermute | solution.py:24
  35.8 4.5 %collective-permute-done.6 = bf16[144,512]{1,0:T(8,128)(2,1)S(1)} collective-permute-done((bf16[144,512]{1,0:T(8,128)(2,1)S(1)}, bf16[144,512]{1,0:T(8,128)(2,1)S(1)}, u32[]{:S(2)}, u32[]{:S(2)}) %collective-permute-start.6) | collective-permute-done | bytes 147488 | tf_op jit(solution)/shard_map/ppermute | solution.py:24
  40.4 2.5 %collective-permute-start.7 = (f32[80,512]{1,0:T(8,128)S(1)}, f32[80,512]{1,0:T(8,128)S(1)}, u32[]{:S(2)}, u32[]{:S(2)}) collective-permute-start(f32[80,512]{1,0:T(8,128)S(1)} %pad_maximum_fusion.8), channel_id=1, source_target_pairs={{0,1},{1,0},{2,3},{3,2},{4,5},{5,4},{6,7},{7,6},{8,9},{9,8},{10,11... | collective-permute-start | bytes 491528 | tf_op jit(solution)/shard_map/ppermute | solution.py:24
  42.9 3.3 %collective-permute-done.7 = f32[80,512]{1,0:T(8,128)S(1)} collective-permute-done((f32[80,512]{1,0:T(8,128)S(1)}, f32[80,512]{1,0:T(8,128)S(1)}, u32[]{:S(2)}, u32[]{:S(2)}) %collective-permute-start.7) | collective-permute-done | bytes 163872 | tf_op jit(solution)/shard_map/ppermute | solution.py:24
  46.3 3.5 %collective-permute-start.8 = (f32[48,512]{1,0:T(8,128)S(1)}, f32[48,512]{1,0:T(8,128)S(1)}, u32[]{:S(2)}, u32[]{:S(2)}) collective-permute-start(f32[48,512]{1,0:T(8,128)S(1)} %pad_maximum_fusion.11), channel_id=1, source_target_pairs={{0,2},{1,3},{2,0},{3,1},{4,6},{5,7},{6,4},{7,5},{8,10},{9,11},{10,... | collective-permute-start | bytes 294920 | tf_op jit(solution)/shard_map/ppermute | solution.py:24
  49.8 2.6 %collective-permute-done.8 = f32[48,512]{1,0:T(8,128)S(1)} collective-permute-done((f32[48,512]{1,0:T(8,128)S(1)}, f32[48,512]{1,0:T(8,128)S(1)}, u32[]{:S(2)}, u32[]{:S(2)}) %collective-permute-start.8) | collective-permute-done | bytes 98336 | tf_op jit(solution)/shard_map/ppermute | solution.py:24
  52.4 0.7 %collective-permute-start.9 = (f32[32,512]{1,0:T(8,128)S(1)}, f32[32,512]{1,0:T(8,128)S(1)}, u32[]{:S(2)}, u32[]{:S(2)}) collective-permute-start(f32[32,512]{1,0:T(8,128)S(1)} %slice_add_fusion), channel_id=1, source_target_pairs={{0,16},{4,20},{8,24},{12,28},{16,0},{20,4},{24,8},{28,12},{1,17},{... | collective-permute-start | bytes 196616 | tf_op jit(solution)/shard_map/ppermute | solution.py:87
  53.2 3.6 %collective-permute-done.9 = f32[32,512]{1,0:T(8,128)S(1)} collective-permute-done((f32[32,512]{1,0:T(8,128)S(1)}, f32[32,512]{1,0:T(8,128)S(1)}, u32[]{:S(2)}, u32[]{:S(2)}) %collective-permute-start.9) | collective-permute-done | bytes 65568 | tf_op jit(solution)/shard_map/ppermute | solution.py:87
  56.8 1.6 %collective-permute-start.10 = (f32[2,32,512]{2,1,0:T(8,128)S(1)}, f32[2,32,512]{2,1,0:T(8,128)S(1)}, u32[]{:S(2)}, u32[]{:S(2)}) collective-permute-start(f32[2,32,512]{2,1,0:T(8,128)S(1)} %pad_maximum_fusion.10), channel_id=1, source_target_pairs={{0,8},{4,12},{8,0},{12,4},{16,24},{20,28},{24,16},{28,20},{1,9},{5... | collective-permute-start | bytes 393224 | tf_op jit(solution)/shard_map/ppermute | solution.py:87
  58.4 3.4 %collective-permute-done.10 = f32[2,32,512]{2,1,0:T(8,128)S(1)} collective-permute-done((f32[2,32,512]{2,1,0:T(8,128)S(1)}, f32[2,32,512]{2,1,0:T(8,128)S(1)}, u32[]{:S(2)}, u32[]{:S(2)}) %collective-permute-start.10) | collective-permute-done | bytes 131104 | tf_op jit(solution)/shard_map/ppermute | solution.py:87
  61.8 0.1 fusion.23
  62.0 0.1 collective-permute-start.11
  62.1 1.5 %collective-permute-done.11 = f32[136,512]{1,0:T(8,128)S(1)} collective-permute-done((f32[136,512]{1,0:T(8,128)S(1)}, f32[136,512]{1,0:T(8,128)S(1)}, u32[]{:S(2)}, u32[]{:S(2)}) %collective-permute-start.11) | collective-permute-done | bytes 278560 | tf_op jit(solution)/shard_map/ppermute | solution.py:24
  63.6 0.1 fusion.18
  63.7 0.8 %copy.40 = f32[2,2,2,32,512]{4,3,2,1,0:T(8,128)} copy(f32[2,2,2,32,512]{4,3,1,0,2:T(8,128)S(1)} %pad_maximum_fusion.3) | data formatting | bytes 1048576 | tf_op jit(solution)/shard_map/stack | solution.py:90
  64.6 0.6 slice_add_fusion.2
  (42 shorter events, 0.7 us)
Async XLA Ops:
  0.6 10.1 %copy-start.4 = (bf16[8,512]{1,0:T(8,128)(2,1)S(1)}, bf16[8,512]{1,0:T(8,128)(2,1)}, u32[]{:S(2)}) copy-start(bf16[8,512]{1,0:T(8,128)(2,1)} %param.8) | copy-start | bytes 24580
  0.6 14.0 %copy-start.2 = (bf16[512,512]{1,0:T(8,128)(2,1)S(1)}, bf16[512,512]{1,0:T(8,128)(2,1)}, u32[]{:S(2)}) copy-start(bf16[512,512]{1,0:T(8,128)(2,1)} %param.7) | copy-start | bytes 1572868
  0.7 11.7 %copy-start = (s32[16,128,128]{2,1,0:T(8,128)S(1)}, s32[16,128,128]{2,1,0:T(8,128)}, u32[]{:S(2)}) copy-start(s32[16,128,128]{2,1,0:T(8,128)} %param.11) | copy-start | bytes 3145732
  0.7 11.7 %copy-start.3 = (s32[512,4]{0,1:T(4,128)S(1)}, s32[512,4]{0,1:T(4,128)}, u32[]{:S(2)}) copy-start(s32[512,4]{0,1:T(4,128)} %param.9) | copy-start | bytes 24580
  0.7 10.1 %collective-permute-start.1 = (bf16[8,512]{1,0:T(8,128)(2,1)}, bf16[8,512]{1,0:T(8,128)(2,1)S(1)}, u32[]{:S(2)}, u32[]{:S(2)}) collective-permute-start(bf16[8,512]{1,0:T(8,128)(2,1)} %param.8), channel_id=1, source_target_pairs={{0,16},{4,20},{8,24},{12,28},{16,0},{20,4},{24,8},{28,12},{1,17},{... | collective-permute-start | bytes 24584 | tf_op jit(solution)/shard_map/ppermute | solution.py:87
  3.7 14.7 %collective-permute-start = (bf16[512,512]{1,0:T(8,128)(2,1)}, bf16[512,512]{1,0:T(8,128)(2,1)}, u32[]{:S(2)}, u32[]{:S(2)}) collective-permute-start(bf16[512,512]{1,0:T(8,128)(2,1)} %param.7), channel_id=1, source_target_pairs={{0,1},{1,2},{2,3},{4,5},{5,6},{6,7},{8,9},{9,10},{10,11},{12,13},{... | collective-permute-start | bytes 1572872 | tf_op jit(solution)/shard_map/ppermute | solution.py:10
  10.8 3.8 %collective-permute-start.2 = (bf16[2,8,512]{2,1,0:T(8,128)(2,1)S(1)}, bf16[2,8,512]{2,1,0:T(8,128)(2,1)S(1)}, u32[]{:S(2)}, u32[]{:S(2)}) collective-permute-start(bf16[2,8,512]{2,1,0:T(8,128)(2,1)S(1)} %pad_maximum_fusion.14), channel_id=1, source_target_pairs={{0,8},{4,12},{8,0},{12,4},{16,24},{20,28},{24,16},{28,20},{1,9},{5... | collective-permute-start | bytes 49160 | tf_op jit(solution)/shard_map/ppermute | solution.py:87
  14.6 1.4 %collective-permute-start.3 = (bf16[2,2,8,512]{3,2,1,0:T(8,128)(2,1)S(1)}, bf16[2,2,8,512]{3,2,1,0:T(8,128)(2,1)S(1)}, u32[]{:S(2)}, u32[]{:S(2)}) collective-permute-start(bf16[2,2,8,512]{3,2,1,0:T(8,128)(2,1)S(1)} %pad_maximum_fusion.13), channel_id=1, source_target_pairs={{0,4},{4,0},{8,12},{12,8},{16,20},{20,16},{24,28},{28,24},{1,5},{5... | collective-permute-start | bytes 98312 | tf_op jit(solution)/shard_map/ppermute | solution.py:87
  19.3 1.2 %copy-start.5 = (bf16[1024,512]{1,0:T(8,128)(2,1)S(1)}, bf16[1024,512]{1,0:T(8,128)(2,1)}, u32[]{:S(2)}) copy-start(bf16[1024,512]{1,0:T(8,128)(2,1)} %param.12) | copy-start | bytes 3145732
  19.3 1.3 %copy-start.6 = (bf16[512,512]{1,0:T(8,128)(2,1)S(1)}, bf16[512,512]{1,0:T(8,128)(2,1)}, u32[]{:S(2)}) copy-start(bf16[512,512]{1,0:T(8,128)(2,1)} %param.13) | copy-start | bytes 1572868
  22.6 0.8 %copy-start.1 = (bf16[512,512]{1,0:T(8,128)(2,1)}, bf16[512,512]{1,0:T(8,128)(2,1)S(1)}, u32[]{:S(2)}) copy-start(bf16[512,512]{1,0:T(8,128)(2,1)S(1)} %get-tuple-element.3) | copy-start | bytes 1572868
  23.4 2.9 %collective-permute-start.4 = (f32[512,512]{1,0:T(8,128)S(1)}, f32[512,512]{1,0:T(8,128)}, u32[]{:S(2)}, u32[]{:S(2)}) collective-permute-start(f32[512,512]{1,0:T(8,128)S(1)} %bitcast.124), channel_id=1, source_target_pairs={{0,4},{4,0},{8,12},{12,8},{16,20},{20,16},{24,28},{28,24},{1,5},{5... | collective-permute-start | bytes 3145736 | tf_op jit(solution)/shard_map/ppermute | solution.py:24
  27.9 6.8 %collective-permute-start.5 = (bf16[288,512]{1,0:T(8,128)(2,1)S(1)}, bf16[288,512]{1,0:T(8,128)(2,1)S(1)}, u32[]{:S(2)}, u32[]{:S(2)}) collective-permute-start(bf16[288,512]{1,0:T(8,128)(2,1)S(1)} %pad_maximum_fusion.4), channel_id=1, source_target_pairs={{0,8},{4,20},{8,0},{12,28},{16,24},{20,4},{24,16},{28,12},{1,9},{5... | collective-permute-start | bytes 884744 | tf_op jit(solution)/shard_map/ppermute | solution.py:24
  35.0 5.2 %collective-permute-start.6 = (bf16[144,512]{1,0:T(8,128)(2,1)S(1)}, bf16[144,512]{1,0:T(8,128)(2,1)S(1)}, u32[]{:S(2)}, u32[]{:S(2)}) collective-permute-start(bf16[144,512]{1,0:T(8,128)(2,1)S(1)} %pad_maximum_fusion.9), channel_id=1, source_target_pairs={{0,16},{4,12},{8,24},{12,4},{16,0},{20,28},{24,8},{28,20},{1,17},{... | collective-permute-start | bytes 442376 | tf_op jit(solution)/shard_map/ppermute | solution.py:24
  40.4 5.8 %collective-permute-start.7 = (f32[80,512]{1,0:T(8,128)S(1)}, f32[80,512]{1,0:T(8,128)S(1)}, u32[]{:S(2)}, u32[]{:S(2)}) collective-permute-start(f32[80,512]{1,0:T(8,128)S(1)} %pad_maximum_fusion.8), channel_id=1, source_target_pairs={{0,1},{1,0},{2,3},{3,2},{4,5},{5,4},{6,7},{7,6},{8,9},{9,8},{10,11... | collective-permute-start | bytes 491528 | tf_op jit(solution)/shard_map/ppermute | solution.py:24
  46.3 6.1 %collective-permute-start.8 = (f32[48,512]{1,0:T(8,128)S(1)}, f32[48,512]{1,0:T(8,128)S(1)}, u32[]{:S(2)}, u32[]{:S(2)}) collective-permute-start(f32[48,512]{1,0:T(8,128)S(1)} %pad_maximum_fusion.11), channel_id=1, source_target_pairs={{0,2},{1,3},{2,0},{3,1},{4,6},{5,7},{6,4},{7,5},{8,10},{9,11},{10,... | collective-permute-start | bytes 294920 | tf_op jit(solution)/shard_map/ppermute | solution.py:24
  52.4 4.3 %collective-permute-start.9 = (f32[32,512]{1,0:T(8,128)S(1)}, f32[32,512]{1,0:T(8,128)S(1)}, u32[]{:S(2)}, u32[]{:S(2)}) collective-permute-start(f32[32,512]{1,0:T(8,128)S(1)} %slice_add_fusion), channel_id=1, source_target_pairs={{0,16},{4,20},{8,24},{12,28},{16,0},{20,4},{24,8},{28,12},{1,17},{... | collective-permute-start | bytes 196616 | tf_op jit(solution)/shard_map/ppermute | solution.py:87
  56.8 5.0 %collective-permute-start.10 = (f32[2,32,512]{2,1,0:T(8,128)S(1)}, f32[2,32,512]{2,1,0:T(8,128)S(1)}, u32[]{:S(2)}, u32[]{:S(2)}) collective-permute-start(f32[2,32,512]{2,1,0:T(8,128)S(1)} %pad_maximum_fusion.10), channel_id=1, source_target_pairs={{0,8},{4,12},{8,0},{12,4},{16,24},{20,28},{24,16},{28,20},{1,9},{5... | collective-permute-start | bytes 393224 | tf_op jit(solution)/shard_map/ppermute | solution.py:87
  62.0 1.6 %collective-permute-start.11 = (f32[136,512]{1,0:T(8,128)S(1)}, f32[136,512]{1,0:T(8,128)S(1)}, u32[]{:S(2)}, u32[]{:S(2)}) collective-permute-start(f32[136,512]{1,0:T(8,128)S(1)} %pad_maximum_fusion.5), channel_id=1, source_target_pairs={{0,4},{4,0},{8,12},{12,8},{16,20},{20,16},{24,28},{28,24},{1,5},{5... | collective-permute-start | bytes 835592 | tf_op jit(solution)/shard_map/ppermute | solution.py:24

commit v4 on v3

--- a/solution.py
+++ b/solution.py
@@ -85,9 +85,8 @@
             rider = keep + got_rider
         else:
             got = lax.ppermute(value, axis, pairs)
-        low = jnp.where(mine == 0, value, got)
-        high = jnp.where(mine == 0, got, value)
-        value = jnp.stack([low, high], axis=len(held))
+        value = jnp.stack([value, value], axis=len(held))
+        value = lax.dynamic_update_index_in_dim(value, got, 1 - mine, axis=len(held))
         held.append(bit)
     natural = [held.index(levels - 1 - k) for k in range(levels)]
     if natural != list(range(levels)):
@@ -107,7 +106,7 @@
     total_hubs = owned * regions
     up = list(range(log2(regions)))
     down = up[::-1]
-    prev = shifted(feats, "dom", 1)[rows - tile :]
+    prev = shifted(feats[rows - tile :], "dom", 1)
     hub_table = gather_ordered(hub_feats, "region", down)[0].reshape(total_hubs, width)
     window = jnp.concatenate([prev, feats], axis=0)
     src = tile_src.reshape(nblk, per_block)

time: 65.5 us -> 65.7 us (level)
  starting transfers between devices: 19.7 us -> 17.3 us
  other arithmetic: 5.27 us -> 6.36 us
  local copies, waits for them, and re-layouts: 4.71 us -> 5.61 us
  waiting for transfers between devices: 28.3 us -> 29 us
    ppermute x5, waiting for transfers between devices: 8.91 us -> 10.6 us  [gather_ordered(): got = lax.ppermute(value, axis, pairs)]
    ppermute x1, waiting for transfers between devices: 1.42 us -> 0.01 us  [shifted(): lax.ppermute(value, axis, [(source, source + steps) for source in range(i...]
    ppermute x6, starting transfers between devices: 8.42 us -> 7.05 us  [exchange(): flat = lax.ppermute(flat, axis, pairs).astype(kind)]
    reduce_sum x2, other arithmetic: 0.36 us -> 1.59 us  [layer(): tile_mask.reshape(nblk, per_block, tile, tile).sum(axis=(1, 3))]
    dynamic_update_slice x0 -> x7, local copies, waits for them, and re-layouts: none -> 0.9 us  [gather_ordered(): lax.dynamic_update_index_in_dim(value, got, 1 - mine, axis=len(held))]
    slice x1, local copies, waits for them, and re-layouts: 0.01 us -> 0.86 us  [layer(): hub_ids[:, slot:slot + 1] == hub_cols]
    another operation x2 -> x3, local copies, waits for them, and re-layouts: 0.86 us -> 0.03 us  [gather_ordered(): value = jnp.stack([value, value], axis=len(held))]
    ppermute x1, starting transfers between devices: 4.28 us -> 3.49 us  [shifted(): lax.ppermute(value, axis, [(source, source + steps) for source in range(i...]
  transfers between devices with their start and end apart: 12 -> 12, of which waited for: 10 -> 10; matrix products, arithmetic and copies ran while one was open for 11% -> 16% of each run, Pallas kernels for 0% -> 0%
where the time goes in v4:
time: 65.7 us; the launch traced here: 65.3 us
  waiting for transfers between devices  29 us (44%)
  starting transfers between devices  17.3 us (26%)
  other arithmetic  6.36 us (10%)
  matrix products  6.06 us (9%)
  local copies, waits for them, and re-layouts  5.61 us (9%)
  between operations  1.09 us (2%)
    ppermute x6, waiting for transfers between devices, exchange(): flat = lax.ppermute(flat, axis, pairs).astype(kind)  18.4 us
    ppermute x5, waiting for transfers between devices, gather_ordered(): got = lax.ppermute(value, axis, pairs)  10.6 us
    ppermute x6, starting transfers between devices, exchange(): flat = lax.ppermute(flat, axis, pairs).astype(kind)  7.05 us
    ppermute x5, starting transfers between devices, gather_ordered(): got = lax.ppermute(value, axis, pairs)  6.71 us
    ppermute x1, starting transfers between devices, shifted(): lax.ppermute(value, axis, [(source, source + steps) for source in range(i...  3.49 us
    dot_general x1, matrix products, layer(): z = jnp.dot(inputs, w_stack, preferred_element_type=jnp.float32)  1.9 us
    dot_general x1, matrix products, layer(): lax.dot_general(counts, sgrad, (((0,), (0,)), ((), ())), preferred_elemen...  1.88 us
    reduce_sum x1, other arithmetic, layer(): links = jnp.where(chosen[:, :, None, :, None], masks, 0).sum(axis=1)  1.87 us
  transfers between devices with their start and end apart: 12, of which 10 were waited for; matrix products, arithmetic and copies ran while one was open for 16% of the time, Pallas kernels for 0%

profile of v4, /device:TPU:0, one launch (start us, length us, event | category | flops | bytes accessed | tf_op | source)
XLA Modules:
  0.0 65.3 jit_solution(13751020376644199754)
XLA Ops:
  0.6 0.0 copy-start.2
  0.6 0.0 copy-start
  0.7 3.1 %collective-permute-start.1 = (bf16[8,512]{1,0:T(8,128)(2,1)}, bf16[8,512]{1,0:T(8,128)(2,1)S(1)}, u32[]{:S(2)}, u32[]{:S(2)}) collective-permute-start(bf16[8,512]{1,0:T(8,128)(2,1)} %param.8), channel_id=1, source_target_pairs={{0,16},{4,20},{8,24},{12,28},{16,0},{20,4},{24,8},{28,12},{1,17},{... | collective-permute-start | bytes 24584 | tf_op jit(solution)/shard_map/ppermute | solution.py:87
  3.7 0.9 %slice.48 = bf16[128,512]{1,0:T(8,128)(2,1)S(1)} slice(bf16[512,512]{1,0:T(8,128)(2,1)} %param.7), slice={[384:512], [0:512]} | slice | bytes 262144 | tf_op jit(solution)/shard_map/slice | solution.py:109
  4.6 3.5 %collective-permute-start = (bf16[128,512]{1,0:T(8,128)(2,1)S(1)}, bf16[128,512]{1,0:T(8,128)(2,1)S(1)}, u32[]{:S(2)}, u32[]{:S(2)}) collective-permute-start(bf16[128,512]{1,0:T(8,128)(2,1)S(1)} %slice.48), channel_id=1, source_target_pairs={{0,1},{1,2},{2,3},{4,5},{5,6},{6,7},{8,9},{9,10},{10,11},{12,13},{... | collective-permute-start | bytes 393224 | tf_op jit(solution)/shard_map/ppermute | solution.py:10
  8.1 0.9 %fusion.25 = (s32[512,1]{0,1:T(1,128)S(1)}, s32[512,1]{0,1:T(1,128)S(1)}, s32[512,1]{0,1:T(1,128)S(1)}, s32[512,1]{0,1:T(1,128)S(1)}) fusion(s32[512,4]{0,1:T(4,128)} %param.9), kind=kLoop, calls=%fused_computation.81 | loop fusion | bytes 16384 | tf_op jit(solution)/shard_map/slice | solution.py:123
  9.0 0.7 %eq.57 = s32[4,4]{1,0:T(4,128)S(1)} reshape(s32[16]{0:T(128)} %param.10) | data formatting | bytes 128 | tf_op jit(solution)/shard_map/eq | solution.py:113
  9.7 0.1 iota_compare_fusion.4
  9.8 1.6 %reduce_sum.26 = s32[16,128]{1,0:T(8,128)S(1)} reduce(s32[16,128,128]{2,1,0:T(8,128)} %param.11, s32[]{:T(128)} %constant.110.clone.1), dimensions={2}, to_apply=%region_1.2 | reduce | flops 260096 | bytes 1056772 | tf_op jit(solution)/shard_map/reduce_sum | solution.py:118
  11.4 1.9 %select_reduce_fusion = s32[4,128,5,128]{3,1,2,0:T(8,128)S(1)} fusion(s32[4,4,128,128]{3,2,1,0:T(8,128)} %bitcast.108, pred[4,4,5]{2,1,0:T(4,128)(4,1)S(1)} %iota_compare_fusion.4), kind=kLoop, calls=%fused_computation | loop fusion | flops 2293760 | bytes 2359376 | tf_op jit(solution)/shard_map/reduce_sum | solution.py:115
  13.3 0.0 copy-done.2
  13.3 0.0 copy-done
  13.3 0.2 copy.34
  13.5 0.1 convert_element_type.56
  13.7 0.9 %copy.31 = bf16[4,128,5,128]{1,0,3,2:T(4,128)(2,1)S(1)} copy(bf16[4,128,5,128]{3,1,2,0:T(8,128)(2,1)S(1)} %convert_element_type.56) | data formatting | bytes 1310720 | tf_op jit(solution)/shard_map/convert_element_type | solution.py:117
  14.6 0.0 collective-permute-done.1
  14.7 1.6 %collective-permute-start.2 = (bf16[2,8,512]{2,1,0:T(8,128)(2,1)S(1)}, bf16[2,8,512]{2,1,0:T(8,128)(2,1)S(1)}, u32[]{:S(2)}, u32[]{:S(2)}) collective-permute-start(bf16[2,8,512]{2,1,0:T(8,128)(2,1)S(1)} %bitcast_dynamic-update-slice_fusion.4), channel_id=1, source_target_pairs={{0,8},{4,12},{8,0},{12,4},{16,24},{20,28},{24,16},{28,20},{1,9},{5... | collective-permute-start | bytes 49160 | tf_op jit(solution)/shard_map/ppermute | solution.py:87
  16.2 2.2 %collective-permute-done.2 = bf16[2,8,512]{2,1,0:T(8,128)(2,1)S(1)} collective-permute-done((bf16[2,8,512]{2,1,0:T(8,128)(2,1)S(1)}, bf16[2,8,512]{2,1,0:T(8,128)(2,1)S(1)}, u32[]{:S(2)}, u32[]{:S(2)}) %collective-permute-start.2) | collective-permute-done | bytes 16416 | tf_op jit(solution)/shard_map/ppermute | solution.py:87
  18.5 0.0 collective-permute-start.3
  18.5 1.2 %collective-permute-done.3 = bf16[2,2,8,512]{3,2,1,0:T(8,128)(2,1)S(1)} collective-permute-done((bf16[2,2,8,512]{3,2,1,0:T(8,128)(2,1)S(1)}, bf16[2,2,8,512]{3,2,1,0:T(8,128)(2,1)S(1)}, u32[]{:S(2)}, u32[]{:S(2)}) %collective-permute-start.3) | collective-permute-done | bytes 32800 | tf_op jit(solution)/shard_map/ppermute | solution.py:87
  19.7 0.9 %fusion.17 = f32[512,512]{0,1:T(8,128)S(1)} fusion(bf16[64,512]{1,0:T(8,128)(2,1)S(1)} %bitcast.126, s32[512]{0:T(512)S(1)} %bitcast.135, s32[512]{0:T(512)S(1)} %bitcast.137, s32[512]{0:T(512)S(1)} %bitcast.133, s32[512]{0:T(512)S(1)} %bitcast.131), kind=kOutput, calls=%fused_computation.43 | convolution fusion | flops 33947648 | bytes 1122304 | tf_op jit(solution)/shard_map/dot_general | solution.py:125
  20.6 0.0 collective-permute-done
  20.6 0.0 copy-start.3
  20.6 0.0 copy-start.4
  20.6 0.7 %fusion.2 = bf16[512,512]{0,1:T(8,128)(2,1)S(1)} fusion(f32[512,512]{0,1:T(8,128)S(1)} %fusion.17, bf16[512,512]{0,1:T(8,128)(2,1)S(1)} %copy.34, bf16[80,8,4,128]{3,2,1,0:T(4,128)(2,1)S(1)} %bitcast.116, bf16[512,512]{1,0:T(8,128)(2,1)S(1)} %copy-done, bf16[128,512]{1,0:T(8,128)(2,1)S(1)} %collective-permute-done, f32[512]{0:T(512)S(1)} %add_bitcast_fusion), kind=kOutput, calls=%fused_computation.5 | convolution fusion | flops 338165760 | bytes 3409920 | tf_op jit(solution)/shard_map/dot_general | solution.py:117
  21.3 0.5 copy-done.3
  21.8 0.1 copy-done.4
  22.0 1.9 %multiply_convert_fusion = (bf16[512,512]{1,0:T(8,128)(2,1)S(1)}, bf16[512,512]{1,0:T(8,128)(2,1)}) fusion(bf16[512,512]{1,0:T(8,128)(2,1)S(1)} %copy-done.4, bf16[1024,512]{1,0:T(8,128)(2,1)S(1)} %copy-done.3, bf16[512,512]{0,1:T(8,128)(2,1)S(1)} %fusion.2, bf16[512,512]{0,1:T(8,128)(2,1)S(1)} %copy.34), kind=kOutput, calls=%fused_computation.10 | convolution fusion | flops 542113792 | bytes 3670016 | tf_op jit(solution)/shard_map/dot_general | solution.py:128
  23.9 0.0 copy-start.1
  23.9 0.7 %fusion.5 = f32[1024,512]{1,0:T(8,128)S(1)} fusion(bf16[512,512]{1,0:T(8,128)(2,1)S(1)} %get-tuple-element.3, bf16[512,512]{0,1:T(8,128)(2,1)S(1)} %fusion.2, bf16[512,512]{0,1:T(8,128)(2,1)S(1)} %copy.34), kind=kOutput, calls=%fused_computation.13 | convolution fusion | flops 538968064 | bytes 3670016 | tf_op jit(solution)/shard_map/dot_general | solution.py:132
  24.6 0.1 constant_dynamic-slice_fusion.5
  24.7 0.0 copy-done.1
  24.7 0.2 collective-permute-start.4
  24.9 1.9 %fusion.4 = f32[64,512]{1,0:T(8,128)S(1)} fusion(bf16[512,512]{1,0:T(8,128)(2,1)} %copy-done.1, bf16[1024,512]{1,0:T(8,128)(2,1)} %param.12, f32[512]{0:T(512)S(1)} %add_bitcast_fusion, s32[512]{0:T(512)S(1)} %bitcast.136, s32[512]{0:T(512)S(1)} %bitcast.138, s32[512]{0:T(512)S(1)} %bitcast.134, s32[512]{0:T(512)S(1)} %bitcast.132), kind=kOutput, calls=%fused_computation.7 | convolution fusion | flops 302907392 | bytes 1189888 | tf_op jit(solution)/shard_map/dot_general | solution.py:139
  26.9 0.7 %collective-permute-done.4 = f32[512,512]{1,0:T(8,128)} collective-permute-done((f32[512,512]{1,0:T(8,128)S(1)}, f32[512,512]{1,0:T(8,128)}, u32[]{:S(2)}, u32[]{:S(2)}) %collective-permute-start.4) | collective-permute-done | bytes 1048608 | tf_op jit(solution)/shard_map/ppermute | solution.py:24
  27.5 1.4 %bitcast_add_fusion = f32[4,2,2,32,512]{4,3,2,1,0:T(8,128)S(1)} fusion(f32[4,2,2,32,512]{4,3,2,1,0:T(8,128)} %bitcast.17, f32[4,2,2,2,32,512]{5,4,3,2,1,0:T(8,128)S(1)} %bitcast.107, s32[]{:T(128)S(6)} %select_n.150), kind=kLoop, calls=%fused_computation.9 | loop fusion | flops 262144 | bytes 3145732 | tf_op jit(solution)/shard_map/add | solution.py:67
  29.1 0.1 fusion.12
  29.2 1.6 %collective-permute-start.5 = (bf16[288,512]{1,0:T(8,128)(2,1)S(1)}, bf16[288,512]{1,0:T(8,128)(2,1)S(1)}, u32[]{:S(2)}, u32[]{:S(2)}) collective-permute-start(bf16[288,512]{1,0:T(8,128)(2,1)S(1)} %pad_maximum_fusion.4), channel_id=1, source_target_pairs={{0,8},{4,20},{8,0},{12,28},{16,24},{20,4},{24,16},{28,12},{1,9},{5... | collective-permute-start | bytes 884744 | tf_op jit(solution)/shard_map/ppermute | solution.py:24
  30.7 5.2 %collective-permute-done.5 = bf16[288,512]{1,0:T(8,128)(2,1)S(1)} collective-permute-done((bf16[288,512]{1,0:T(8,128)(2,1)S(1)}, bf16[288,512]{1,0:T(8,128)(2,1)S(1)}, u32[]{:S(2)}, u32[]{:S(2)}) %collective-permute-start.5) | collective-permute-done | bytes 294944 | tf_op jit(solution)/shard_map/ppermute | solution.py:24
  36.0 0.1 slice.64
  36.1 0.2 fusion.13
  36.3 0.6 collective-permute-start.6
  36.9 4.6 %collective-permute-done.6 = bf16[144,512]{1,0:T(8,128)(2,1)S(1)} collective-permute-done((bf16[144,512]{1,0:T(8,128)(2,1)S(1)}, bf16[144,512]{1,0:T(8,128)(2,1)S(1)}, u32[]{:S(2)}, u32[]{:S(2)}) %collective-permute-start.6) | collective-permute-done | bytes 147488 | tf_op jit(solution)/shard_map/ppermute | solution.py:24
  41.7 1.6 %collective-permute-start.7 = (f32[80,512]{1,0:T(8,128)S(1)}, f32[80,512]{1,0:T(8,128)S(1)}, u32[]{:S(2)}, u32[]{:S(2)}) collective-permute-start(f32[80,512]{1,0:T(8,128)S(1)} %pad_maximum_fusion.7), channel_id=1, source_target_pairs={{0,1},{1,0},{2,3},{3,2},{4,5},{5,4},{6,7},{7,6},{8,9},{9,8},{10,11... | collective-permute-start | bytes 491528 | tf_op jit(solution)/shard_map/ppermute | solution.py:24
  43.3 3.7 %collective-permute-done.7 = f32[80,512]{1,0:T(8,128)S(1)} collective-permute-done((f32[80,512]{1,0:T(8,128)S(1)}, f32[80,512]{1,0:T(8,128)S(1)}, u32[]{:S(2)}, u32[]{:S(2)}) %collective-permute-start.7) | collective-permute-done | bytes 163872 | tf_op jit(solution)/shard_map/ppermute | solution.py:24
  47.2 3.0 %collective-permute-start.8 = (f32[48,512]{1,0:T(8,128)S(1)}, f32[48,512]{1,0:T(8,128)S(1)}, u32[]{:S(2)}, u32[]{:S(2)}) collective-permute-start(f32[48,512]{1,0:T(8,128)S(1)} %pad_maximum_fusion.10), channel_id=1, source_target_pairs={{0,2},{1,3},{2,0},{3,1},{4,6},{5,7},{6,4},{7,5},{8,10},{9,11},{10,... | collective-permute-start | bytes 294920 | tf_op jit(solution)/shard_map/ppermute | solution.py:24
  50.2 2.6 %collective-permute-done.8 = f32[48,512]{1,0:T(8,128)S(1)} collective-permute-done((f32[48,512]{1,0:T(8,128)S(1)}, f32[48,512]{1,0:T(8,128)S(1)}, u32[]{:S(2)}, u32[]{:S(2)}) %collective-permute-start.8) | collective-permute-done | bytes 98336 | tf_op jit(solution)/shard_map/ppermute | solution.py:24
  52.8 0.5 collective-permute-start.9
  53.4 3.7 %collective-permute-done.9 = f32[32,512]{1,0:T(8,128)S(1)} collective-permute-done((f32[32,512]{1,0:T(8,128)S(1)}, f32[32,512]{1,0:T(8,128)S(1)}, u32[]{:S(2)}, u32[]{:S(2)}) %collective-permute-start.9) | collective-permute-done | bytes 65568 | tf_op jit(solution)/shard_map/ppermute | solution.py:87
  57.1 1.5 %collective-permute-start.10 = (f32[2,32,512]{2,1,0:T(8,128)S(1)}, f32[2,32,512]{2,1,0:T(8,128)S(1)}, u32[]{:S(2)}, u32[]{:S(2)}) collective-permute-start(f32[2,32,512]{2,1,0:T(8,128)S(1)} %bitcast_dynamic-update-slice_fusion.1), channel_id=1, source_target_pairs={{0,8},{4,12},{8,0},{12,4},{16,24},{20,28},{24,16},{28,20},{1,9},{5... | collective-permute-start | bytes 393224 | tf_op jit(solution)/shard_map/ppermute | solution.py:87
  58.7 3.4 %collective-permute-done.10 = f32[2,32,512]{2,1,0:T(8,128)S(1)} collective-permute-done((f32[2,32,512]{2,1,0:T(8,128)S(1)}, f32[2,32,512]{2,1,0:T(8,128)S(1)}, u32[]{:S(2)}, u32[]{:S(2)}) %collective-permute-start.10) | collective-permute-done | bytes 131104 | tf_op jit(solution)/shard_map/ppermute | solution.py:87
  62.2 0.1 collective-permute-start.11
  62.3 0.1 pad_maximum_fusion.3
  62.4 1.5 %collective-permute-done.11 = f32[136,512]{1,0:T(8,128)S(1)} collective-permute-done((f32[136,512]{1,0:T(8,128)S(1)}, f32[136,512]{1,0:T(8,128)S(1)}, u32[]{:S(2)}, u32[]{:S(2)}) %collective-permute-start.11) | collective-permute-done | bytes 278560 | tf_op jit(solution)/shard_map/ppermute | solution.py:24
  63.9 0.8 %copy.37 = f32[2,2,2,32,512]{4,3,2,1,0:T(8,128)} copy(f32[2,2,2,32,512]{4,3,1,0,2:T(8,128)S(1)} %constant_dynamic-update-slice_fusion) | data formatting | bytes 1048576 | tf_op jit(solution)/shard_map/jit(dynamic_update_index_in_dim)/dynamic_update_slice | solution.py:89
  64.7 0.6 slice_add_fusion.2
  (44 shorter events, 0.7 us)
Async XLA Ops:
  0.6 12.7 %copy-start.2 = (bf16[8,512]{1,0:T(8,128)(2,1)S(1)}, bf16[8,512]{1,0:T(8,128)(2,1)}, u32[]{:S(2)}) copy-start(bf16[8,512]{1,0:T(8,128)(2,1)} %param.8) | copy-start | bytes 24580
  0.6 12.7 %copy-start = (bf16[512,512]{1,0:T(8,128)(2,1)S(1)}, bf16[512,512]{1,0:T(8,128)(2,1)}, u32[]{:S(2)}) copy-start(bf16[512,512]{1,0:T(8,128)(2,1)} %param.7) | copy-start | bytes 1572868
  0.7 14.0 %collective-permute-start.1 = (bf16[8,512]{1,0:T(8,128)(2,1)}, bf16[8,512]{1,0:T(8,128)(2,1)S(1)}, u32[]{:S(2)}, u32[]{:S(2)}) collective-permute-start(bf16[8,512]{1,0:T(8,128)(2,1)} %param.8), channel_id=1, source_target_pairs={{0,16},{4,20},{8,24},{12,28},{16,0},{20,4},{24,8},{28,12},{1,17},{... | collective-permute-start | bytes 24584 | tf_op jit(solution)/shard_map/ppermute | solution.py:87
  4.6 16.0 %collective-permute-start = (bf16[128,512]{1,0:T(8,128)(2,1)S(1)}, bf16[128,512]{1,0:T(8,128)(2,1)S(1)}, u32[]{:S(2)}, u32[]{:S(2)}) collective-permute-start(bf16[128,512]{1,0:T(8,128)(2,1)S(1)} %slice.48), channel_id=1, source_target_pairs={{0,1},{1,2},{2,3},{4,5},{5,6},{6,7},{8,9},{9,10},{10,11},{12,13},{... | collective-permute-start | bytes 393224 | tf_op jit(solution)/shard_map/ppermute | solution.py:10
  14.7 3.8 %collective-permute-start.2 = (bf16[2,8,512]{2,1,0:T(8,128)(2,1)S(1)}, bf16[2,8,512]{2,1,0:T(8,128)(2,1)S(1)}, u32[]{:S(2)}, u32[]{:S(2)}) collective-permute-start(bf16[2,8,512]{2,1,0:T(8,128)(2,1)S(1)} %bitcast_dynamic-update-slice_fusion.4), channel_id=1, source_target_pairs={{0,8},{4,12},{8,0},{12,4},{16,24},{20,28},{24,16},{28,20},{1,9},{5... | collective-permute-start | bytes 49160 | tf_op jit(solution)/shard_map/ppermute | solution.py:87
  18.5 1.2 %collective-permute-start.3 = (bf16[2,2,8,512]{3,2,1,0:T(8,128)(2,1)S(1)}, bf16[2,2,8,512]{3,2,1,0:T(8,128)(2,1)S(1)}, u32[]{:S(2)}, u32[]{:S(2)}) collective-permute-start(bf16[2,2,8,512]{3,2,1,0:T(8,128)(2,1)S(1)} %bitcast_dynamic-update-slice_fusion.3), channel_id=1, source_target_pairs={{0,4},{4,0},{8,12},{12,8},{16,20},{20,16},{24,28},{28,24},{1,5},{5... | collective-permute-start | bytes 98312 | tf_op jit(solution)/shard_map/ppermute | solution.py:87
  20.6 1.2 %copy-start.3 = (bf16[1024,512]{1,0:T(8,128)(2,1)S(1)}, bf16[1024,512]{1,0:T(8,128)(2,1)}, u32[]{:S(2)}) copy-start(bf16[1024,512]{1,0:T(8,128)(2,1)} %param.12) | copy-start | bytes 3145732
  20.6 1.3 %copy-start.4 = (bf16[512,512]{1,0:T(8,128)(2,1)S(1)}, bf16[512,512]{1,0:T(8,128)(2,1)}, u32[]{:S(2)}) copy-start(bf16[512,512]{1,0:T(8,128)(2,1)} %param.13) | copy-start | bytes 1572868
  23.9 0.8 %copy-start.1 = (bf16[512,512]{1,0:T(8,128)(2,1)}, bf16[512,512]{1,0:T(8,128)(2,1)S(1)}, u32[]{:S(2)}) copy-start(bf16[512,512]{1,0:T(8,128)(2,1)S(1)} %get-tuple-element.3) | copy-start | bytes 1572868
  24.7 2.9 %collective-permute-start.4 = (f32[512,512]{1,0:T(8,128)S(1)}, f32[512,512]{1,0:T(8,128)}, u32[]{:S(2)}, u32[]{:S(2)}) collective-permute-start(f32[512,512]{1,0:T(8,128)S(1)} %bitcast.112), channel_id=1, source_target_pairs={{0,4},{4,0},{8,12},{12,8},{16,20},{20,16},{24,28},{28,24},{1,5},{5... | collective-permute-start | bytes 3145736 | tf_op jit(solution)/shard_map/ppermute | solution.py:24
  29.2 6.8 %collective-permute-start.5 = (bf16[288,512]{1,0:T(8,128)(2,1)S(1)}, bf16[288,512]{1,0:T(8,128)(2,1)S(1)}, u32[]{:S(2)}, u32[]{:S(2)}) collective-permute-start(bf16[288,512]{1,0:T(8,128)(2,1)S(1)} %pad_maximum_fusion.4), channel_id=1, source_target_pairs={{0,8},{4,20},{8,0},{12,28},{16,24},{20,4},{24,16},{28,12},{1,9},{5... | collective-permute-start | bytes 884744 | tf_op jit(solution)/shard_map/ppermute | solution.py:24
  36.3 5.2 %collective-permute-start.6 = (bf16[144,512]{1,0:T(8,128)(2,1)S(1)}, bf16[144,512]{1,0:T(8,128)(2,1)S(1)}, u32[]{:S(2)}, u32[]{:S(2)}) collective-permute-start(bf16[144,512]{1,0:T(8,128)(2,1)S(1)} %pad_maximum_fusion.8), channel_id=1, source_target_pairs={{0,16},{4,12},{8,24},{12,4},{16,0},{20,28},{24,8},{28,20},{1,17},{... | collective-permute-start | bytes 442376 | tf_op jit(solution)/shard_map/ppermute | solution.py:24
  41.7 5.4 %collective-permute-start.7 = (f32[80,512]{1,0:T(8,128)S(1)}, f32[80,512]{1,0:T(8,128)S(1)}, u32[]{:S(2)}, u32[]{:S(2)}) collective-permute-start(f32[80,512]{1,0:T(8,128)S(1)} %pad_maximum_fusion.7), channel_id=1, source_target_pairs={{0,1},{1,0},{2,3},{3,2},{4,5},{5,4},{6,7},{7,6},{8,9},{9,8},{10,11... | collective-permute-start | bytes 491528 | tf_op jit(solution)/shard_map/ppermute | solution.py:24
  47.2 5.6 %collective-permute-start.8 = (f32[48,512]{1,0:T(8,128)S(1)}, f32[48,512]{1,0:T(8,128)S(1)}, u32[]{:S(2)}, u32[]{:S(2)}) collective-permute-start(f32[48,512]{1,0:T(8,128)S(1)} %pad_maximum_fusion.10), channel_id=1, source_target_pairs={{0,2},{1,3},{2,0},{3,1},{4,6},{5,7},{6,4},{7,5},{8,10},{9,11},{10,... | collective-permute-start | bytes 294920 | tf_op jit(solution)/shard_map/ppermute | solution.py:24
  52.8 4.3 %collective-permute-start.9 = (f32[32,512]{1,0:T(8,128)S(1)}, f32[32,512]{1,0:T(8,128)S(1)}, u32[]{:S(2)}, u32[]{:S(2)}) collective-permute-start(f32[32,512]{1,0:T(8,128)S(1)} %slice_add_fusion), channel_id=1, source_target_pairs={{0,16},{4,20},{8,24},{12,28},{16,0},{20,4},{24,8},{28,12},{1,17},{... | collective-permute-start | bytes 196616 | tf_op jit(solution)/shard_map/ppermute | solution.py:87
  57.1 5.0 %collective-permute-start.10 = (f32[2,32,512]{2,1,0:T(8,128)S(1)}, f32[2,32,512]{2,1,0:T(8,128)S(1)}, u32[]{:S(2)}, u32[]{:S(2)}) collective-permute-start(f32[2,32,512]{2,1,0:T(8,128)S(1)} %bitcast_dynamic-update-slice_fusion.1), channel_id=1, source_target_pairs={{0,8},{4,12},{8,0},{12,4},{16,24},{20,28},{24,16},{28,20},{1,9},{5... | collective-permute-start | bytes 393224 | tf_op jit(solution)/shard_map/ppermute | solution.py:87
  62.2 1.6 %collective-permute-start.11 = (f32[136,512]{1,0:T(8,128)S(1)}, f32[136,512]{1,0:T(8,128)S(1)}, u32[]{:S(2)}, u32[]{:S(2)}) collective-permute-start(f32[136,512]{1,0:T(8,128)S(1)} %pad_maximum_fusion.5), channel_id=1, source_target_pairs={{0,4},{4,0},{8,12},{12,8},{16,20},{20,16},{24,28},{28,24},{1,5},{5... | collective-permute-start | bytes 835592 | tf_op jit(solution)/shard_map/ppermute | solution.py:24
